TPU v7x, 512 devices: a whole 4x8x8 slice. The times are simulated.
512 devices in a mesh: dp: 8 (over z_hi, core), seq: 64 (over x, z_lo, y).
Axes of the slice: x: 4, y: 8, z: 8 (z_hi: 4, z_lo: 2; z = z_hi * 2 + z_lo), core: 2. Of those that a mesh axis runs over, the one named last changes fastest.
Arguments:
- y_first: bfloat16 [8, 128, 64, 1152], P('dp', 'seq'), may hold values from -10 to 10
- y_second: bfloat16 [8, 128, 64, 1152], P('dp', 'seq'), may hold values from -10 to 10
- grad_first: bfloat16 [8, 128, 64, 1152], P('dp', 'seq'), may hold values from -6 to 6
- grad_second: bfloat16 [8, 128, 64, 1152], P('dp', 'seq'), may hold values from -6 to 6
- w_qkv_space: bfloat16 [1152, 1728], P('seq', 'dp'), may hold values from -1 to 1
- w_out_space: bfloat16 [576, 1152], P('seq', 'dp'), may hold values from -0.25 to 0.25
- w_qkv_time: bfloat16 [1152, 1728], P('seq', 'dp'), may hold values from -1 to 1
- w_out_time: bfloat16 [576, 1152], P('seq', 'dp'), may hold values from -0.25 to 0.25
Outputs:
- x_first: bfloat16 [8, 128, 64, 1152], P('dp', 'seq')
- x_second: bfloat16 [8, 128, 64, 1152], P('dp', 'seq')
- d_first: bfloat16 [8, 128, 64, 1152], P('dp', 'seq')
- d_second: bfloat16 [8, 128, 64, 1152], P('dp', 'seq')
- grad_w_out_time: float32 [576, 1152], P('seq', 'dp')
All inputs are finite; a program needn't handle non-finite values.
Results may differ from a plain program's by a relative error of at most 0.025.
Values may be sent and summed in bfloat16 or wider, within the bound.
No kernel may reach another device: no remote copies, remote signals or barrier semaphores. Data moves between devices by JAX's collectives and lax.ppermute only.
A program may use at most 64 MiB of HBM per device.

v0:
```python
import math

import jax
import jax.numpy as jnp
from jax import lax
from jax.sharding import PartitionSpec as P

HEADS = 8
HD = 72


def for_sending(shard):

    def short(part):
        return part.astype(jnp.bfloat16) if part.dtype == jnp.float32 else part

    return jax.tree.map(short, shard)


def normalize(values):
    wide = values.astype(jnp.float32)
    scale = lax.rsqrt(jnp.mean(wide * wide, axis=-1, keepdims=True) + 1e-06)
    return (wide * scale).astype(jnp.bfloat16)


def attend(inputs, w_qkv, w_out):
    outer, rows, inner, width = inputs.shape
    normed = normalize(inputs).reshape(-1, width)
    packed = jnp.dot(normed, w_qkv, preferred_element_type=jnp.float32).astype(jnp.bfloat16)
    packed = packed.reshape(outer, rows, inner, 3, HEADS, HD)
    query = packed[:, :, :, 0]
    keys = packed[:, :, :, 1]
    values = packed[:, :, :, 2]
    scores = jnp.einsum(
        "arbhk,asbhk->abhrs", query, keys, preferred_element_type=jnp.float32
    ) / math.sqrt(HD)
    peak = jnp.max(scores, axis=-1, keepdims=True)
    expo = jnp.exp(scores - peak)
    probs = (expo / jnp.sum(expo, axis=-1, keepdims=True)).astype(jnp.bfloat16)
    mixed = jnp.einsum(
        "abhrs,asbhk->arbhk", probs, values, preferred_element_type=jnp.float32
    ).astype(jnp.bfloat16)
    mixed = mixed.reshape(outer, rows, inner, HEADS * HD)
    result = jnp.dot(
        mixed.reshape(-1, HEADS * HD), w_out, preferred_element_type=jnp.float32
    ).astype(jnp.bfloat16)
    return (result.reshape(inputs.shape), mixed)


def body(
    y_first, y_second, grad_first, grad_second, w_qkv_space, w_out_space, w_qkv_time, w_out_time
):
    part_a, part_b, part_c, part_d = (
        lax.all_gather(w_qkv_space, "seq", axis=0, tiled=True),
        lax.all_gather(w_out_space, "seq", axis=0, tiled=True),
        lax.all_gather(w_qkv_time, "seq", axis=0, tiled=True),
        lax.all_gather(w_out_time, "seq", axis=0, tiled=True),
    )
    space_qkv, space_proj, time_qkv, time_proj = (
        lax.all_gather(part_a, "dp", axis=1, tiled=True),
        lax.all_gather(part_b, "dp", axis=1, tiled=True),
        lax.all_gather(part_c, "dp", axis=1, tiled=True),
        lax.all_gather(part_d, "dp", axis=1, tiled=True),
    )
    frame_count = y_first.shape[1]
    tokens = y_first.shape[2]
    width = y_first.shape[3]

    def time_fn(inputs):
        return attend(inputs, time_qkv, time_proj)

    def space_fn(inputs):
        return attend(inputs, space_qkv, space_proj)[0]

    first_patch = lax.all_to_all(y_first, "seq", split_axis=2, concat_axis=1, tiled=True)
    time_out, time_vjp, time_mixed = jax.vjp(time_fn, first_patch, has_aux=True)
    time_frames = jax.tree.map(
        lambda part, own: part.astype(own.dtype),
        lax.all_to_all(for_sending(time_out), "seq", split_axis=1, concat_axis=2, tiled=True),
        time_out,
    )
    second_in = (y_second.astype(jnp.float32) - time_frames.astype(jnp.float32)).astype(
        jnp.bfloat16
    )
    space_out, space_vjp = jax.vjp(space_fn, second_in.reshape(frame_count, tokens, 1, width))
    first_in = (
        y_first.astype(jnp.float32) - space_out.reshape(y_first.shape).astype(jnp.float32)
    ).astype(jnp.bfloat16)
    cot_patch = lax.all_to_all(grad_second, "seq", split_axis=2, concat_axis=1, tiled=True)
    back_patch = time_vjp(cot_patch)[0]
    back_frames = jax.tree.map(
        lambda part, own: part.astype(own.dtype),
        lax.all_to_all(for_sending(back_patch), "seq", split_axis=1, concat_axis=2, tiled=True),
        back_patch,
    )
    first_grad = (grad_first.astype(jnp.float32) + back_frames.astype(jnp.float32)).astype(
        jnp.bfloat16
    )
    back_space = space_vjp(first_grad.reshape(frame_count, tokens, 1, width))[0]
    second_grad = (
        grad_second.astype(jnp.float32) + back_space.reshape(y_first.shape).astype(jnp.float32)
    ).astype(jnp.bfloat16)
    partial_grad = lax.dot_general(
        time_mixed.reshape(-1, time_mixed.shape[3]),
        cot_patch.reshape(-1, width),
        (((0,), (0,)), ((), ())),
        preferred_element_type=jnp.float32,
    )
    row_share = lax.psum_scatter(partial_grad, "seq", scatter_dimension=0, tiled=True)
    grad_share = lax.psum_scatter(
        row_share.astype(jnp.bfloat16), "dp", scatter_dimension=1, tiled=True
    ).astype(jnp.float32)
    return (first_in, second_in, first_grad, second_grad, grad_share)


def solution(mesh):
    placed = (
        P("dp", "seq", None, None),
        P("dp", "seq", None, None),
        P("dp", "seq", None, None),
        P("dp", "seq", None, None),
        P("seq", "dp"),
        P("seq", "dp"),
        P("seq", "dp"),
        P("seq", "dp"),
    )
    return jax.shard_map(
        body,
        mesh=mesh,
        in_specs=placed,
        out_specs=(
            P("dp", "seq", None, None),
            P("dp", "seq", None, None),
            P("dp", "seq", None, None),
            P("dp", "seq", None, None),
            P("seq", "dp"),
        ),
        check_vma=False,
    )
```

profile of v0, /device:TPU:1, one launch (start us, length us, event | category | flops | bytes accessed | tf_op | source)
XLA Modules:
  0.0 1113.6 jit_solution(6876074772628245804)
XLA Ops:
  7.2 133.8 %all-gather.1 = bf16[64,9,144]{2,1,0:T(8,128)(2,1)S(1)} all-gather(bf16[1,9,144]{2,1,0:T(8,128)(2,1)} %bitcast.214), channel_id=1, replica_groups=mesh['dp'=8,'seq'=64] {'seq'}, dimensions={0}, use_global_device_ids=true | all-gather | bytes 168480 | tf_op jit(solution)/shard_map/all_gather | solution.py:57
  141.2 0.8 copy.137
  142.1 127.3 %all-gather = bf16[64,18,216]{2,1,0:T(8,128)(2,1)S(1)} all-gather(bf16[1,18,216]{2,1,0:T(8,128)(2,1)} %bitcast.212), channel_id=1, replica_groups=mesh['dp'=8,'seq'=64] {'seq'}, dimensions={0}, use_global_device_ids=true | all-gather | bytes 505440 | tf_op jit(solution)/shard_map/all_gather | solution.py:56
  269.7 1.0 copy.135
  270.8 1.0 copy.132
  271.8 4.6 all-to-all-start
  276.4 1.0 copy.148
  277.4 1.3 dynamic-slice
  279.4 8.3 all-to-all-done
  287.7 4.6 all-to-all-start.2
  293.8 9.9 all-to-all-done.2
  303.8 2.0 convolution_convert_fusion.17
  305.8 75.2 %all-gather.9.cloned.1.call-done = bf16[1152,1728]{0,1:T(8,128)(2,1)} async-done(((bf16[1152,216]{0,1:T(8,128)(2,1)}), bf16[1152,1728]{0,1:T(8,128)(2,1)}) %all-gather.9.cloned.1.call-update) | async-done | bytes 3981328 | tf_op jit(solution)/shard_map/all_gather | solution.py:62
  381.0 3.4 convolution_convert_fusion.3
  384.8 1.6 convert_reduce_fusion.1
  386.5 1.0 fusion.55
  388.1 0.7 copy-done.8
  389.3 287.2 %all-reduce.8 = bf16[576,1152]{1,0:T(8,128)(2,1)} all-reduce(f32[576,1152]{1,0:T(8,128)S(1)} %fusion.60), channel_id=2, replica_groups=mesh['dp'=8,'seq'=64] {'seq'}, use_global_device_ids=true, to_apply=%region_14.0.clone | all-reduce | flops 663552 | bytes 3981312
  676.5 0.8 dynamic-slice_convert_fusion
  677.3 0.9 copy.165
  678.3 125.7 %all-gather.3 = bf16[64,9,144]{2,1,0:T(8,128)(2,1)S(1)} all-gather(bf16[1,9,144]{2,1,0:T(8,128)(2,1)} %bitcast.215), channel_id=1, replica_groups=mesh['dp'=8,'seq'=64] {'seq'}, dimensions={0}, use_global_device_ids=true | all-gather | bytes 168480 | tf_op jit(solution)/shard_map/all_gather | solution.py:55
  804.2 0.8 copy.147
  805.1 129.5 %all-gather.2 = bf16[64,18,216]{2,1,0:T(8,128)(2,1)S(1)} all-gather(bf16[1,18,216]{2,1,0:T(8,128)(2,1)S(1)} %bitcast.213), channel_id=1, replica_groups=mesh['dp'=8,'seq'=64] {'seq'}, dimensions={0}, use_global_device_ids=true | all-gather | bytes 505440 | tf_op jit(solution)/shard_map/all_gather | solution.py:54
  935.0 1.0 copy.140
  937.0 3.0 multiply_reduce_fusion
  940.8 0.5 broadcast.221
  941.3 2.4 reduce.29
  943.7 0.8 reshape.522
  944.5 4.6 all-to-all-start.3
  949.2 0.6 fusion.2
  950.2 2.4 reduce.28
  952.6 0.8 reshape.520
  953.5 0.8 copy.166
  954.3 0.6 convert_element_type.411
  954.9 5.3 all-to-all-done.3
  960.3 5.6 all-to-all-start.1
  966.1 0.6 convert.16
  966.9 2.2 convolution_convert_fusion.16
  969.5 7.3 all-to-all-done.1
  977.0 0.6 convert.14
  978.0 115.5 %all-gather.13.cloned.1.call-done = bf16[1152,1728]{0,1:T(8,128)(2,1)} async-done(((bf16[1152,216]{0,1:T(8,128)(2,1)}), bf16[1152,1728]{0,1:T(8,128)(2,1)}) %all-gather.13.cloned.1.call-update) | async-done | bytes 3981328 | tf_op jit(solution)/shard_map/all_gather | solution.py:60
  1093.5 3.3 convolution_convert_fusion.2
  1097.2 0.6 fusion.57
  1100.7 0.5 copy.158
  1101.2 0.5 reshape.496
  1101.8 3.0 fusion
  1105.4 0.6 convolution_convert_fusion.4
  1106.0 1.1 fusion.16
  (121 shorter events, 11.6 us)
Async XLA Ops:
  7.2 296.6 %all-gather.11.cloned.1.call-start = ((), (), s32[]{:S(2)}) async-start(), calls=%async_computation.6 | async-start | bytes 1658880 | tf_op jit(solution)/shard_map/all_gather | solution.py:63
  141.0 129.8 %copy-start.10 = (bf16[1,2,64,1152]{3,2,1,0:T(8,128)(2,1)S(1)}, bf16[1,2,64,1152]{3,2,1,0:T(8,128)(2,1)}, u32[]{:S(2)}) copy-start(bf16[1,2,64,1152]{3,2,1,0:T(8,128)(2,1)} %param.8) | copy-start | bytes 884740
  142.0 134.4 %copy-start.12 = (bf16[1,2,64,1152]{3,2,1,0:T(8,128)(2,1)S(1)}, bf16[1,2,64,1152]{3,2,1,0:T(8,128)(2,1)}, u32[]{:S(2)}) copy-start(bf16[1,2,64,1152]{3,2,1,0:T(8,128)(2,1)} %param.11) | copy-start | bytes 884740
  142.0 239.0 %all-gather.9.cloned.1.call-start = ((), (), s32[]{:S(2)}) async-start(), calls=%async_computation.5 | async-start | bytes 4478976 | tf_op jit(solution)/shard_map/all_gather | solution.py:62
  271.8 15.9 %all-to-all-start = ((bf16[1,2,64,1152]{3,1,0,2:T(2,128)(2,1)}), bf16[1,2,64,1152]{3,1,0,2:T(2,128)(2,1)S(1)}, u32[]{:S(2)}, u32[]{:S(2)}) async-start(bf16[1,2,64,1152]{3,1,0,2:T(2,128)(2,1)} %copy.132), calls=%async_computation | async-start | bytes 589824 | tf_op jit(solution)/shard_map/all_to_all | solution.py:75
  287.7 15.9 %all-to-all-start.2 = ((bf16[1,2,64,1152]{3,1,0,2:T(2,128)(2,1)}), bf16[1,2,64,1152]{3,1,0,2:T(2,128)(2,1)S(1)}, u32[]{:S(2)}, u32[]{:S(2)}) async-start(bf16[1,2,64,1152]{3,1,0,2:T(2,128)(2,1)} %copy.148), calls=%async_computation.2 | async-start | bytes 589824 | tf_op jit(solution)/shard_map/all_to_all | solution.py:89
  292.3 661.1 %reduce-scatter.4.cloned.1.call-start = ((), (), s32[]{:S(2)}) async-start(), calls=%async_computation.9 | async-start | bytes 331776
  293.7 9.9 copy-start.24
  293.7 90.7 %copy-start.22 = (f32[128]{0:T(128)}, f32[128]{0:T(128)S(1)}, u32[]{:S(2)}) copy-start(f32[128]{0:T(128)S(1)} %rsqrt.26) | copy-start | bytes 1540
  305.8 79.0 %copy-start.15 = (bf16[128,576]{0,1:T(8,128)(2,1)}, bf16[128,576]{0,1:T(8,128)(2,1)S(1)}, u32[]{:S(2)}) copy-start(bf16[128,576]{0,1:T(8,128)(2,1)S(1)} %convolution_convert_fusion.17) | copy-start | bytes 442372
  384.4 3.3 copy-start.4
  387.4 0.7 copy-start.6
  388.1 0.7 copy-start.8
  389.3 415.9 %copy-start.20 = (bf16[18,216]{1,0:T(8,128)(2,1)S(1)}, bf16[18,216]{1,0:T(8,128)(2,1)}, u32[]{:S(2)}) copy-start(bf16[18,216]{1,0:T(8,128)(2,1)} %param.12) | copy-start | bytes 23332
  678.2 288.6 %all-gather.15.cloned.1.call-start = ((), (), s32[]{:S(2)}) async-start(), calls=%async_computation.8 | async-start | bytes 1658880 | tf_op jit(solution)/shard_map/all_gather | solution.py:61
  804.0 132.1 %copy-start.7 = (bf16[8,128,128]{1,2,0:T(8,128)(2,1)S(1)}, bf16[8,128,128]{1,2,0:T(8,128)(2,1)}, u32[]{:S(2)}) copy-start(bf16[8,128,128]{1,2,0:T(8,128)(2,1)} %copy-done.6) | copy-start | bytes 786436
  804.0 132.1 %copy-start.16 = (bf16[128,576]{0,1:T(8,128)(2,1)S(1)}, bf16[128,576]{0,1:T(8,128)(2,1)}, u32[]{:S(2)}) copy-start(bf16[128,576]{0,1:T(8,128)(2,1)} %copy-done.15) | copy-start | bytes 442372
  804.2 132.1 %copy-start.21 = (f32[8,128]{1,0:T(8,128)S(1)}, f32[8,128]{1,0:T(8,128)}, u32[]{:S(2)}) copy-start(f32[8,128]{1,0:T(8,128)} %get-tuple-element.11) | copy-start | bytes 12292
  804.2 132.2 %copy-start.2 = (f32[8,128,128]{1,2,0:T(8,128)S(1)}, f32[8,128,128]{1,2,0:T(8,128)}, u32[]{:S(2)}) copy-start(f32[8,128,128]{1,2,0:T(8,128)} %get-tuple-element.10) | copy-start | bytes 1572868
  804.2 132.2 %copy-start.5 = (bf16[128,1728]{0,1:T(8,128)(2,1)S(1)}, bf16[128,1728]{0,1:T(8,128)(2,1)}, u32[]{:S(2)}) copy-start(bf16[128,1728]{0,1:T(8,128)(2,1)} %copy-done.4) | copy-start | bytes 1327108
  804.2 132.2 %copy-start.17 = (pred[8,128,128]{1,2,0:T(32,128)(4,1)S(1)}, pred[8,128,128]{1,2,0:T(32,128)(4,1)}, u32[]{:S(2)}) copy-start(pred[8,128,128]{1,2,0:T(32,128)(4,1)} %get-tuple-element.12) | copy-start | bytes 393220
  805.1 288.4 %all-gather.13.cloned.1.call-start = ((), (), s32[]{:S(2)}) async-start(), calls=%async_computation.7 | async-start | bytes 4478976 | tf_op jit(solution)/shard_map/all_gather | solution.py:60
  937.0 3.1 copy-start.25
  937.0 3.1 copy-start.23
  940.1 9.1 copy-start.1
  940.1 9.1 copy-start.9
  944.5 15.8 %all-to-all-start.3 = ((bf16[64,2,1152]{2,1,0:T(2,128)(2,1)}), bf16[64,2,1152]{2,1,0:T(2,128)(2,1)S(1)}, u32[]{:S(2)}, u32[]{:S(2)}) async-start(bf16[64,2,1152]{2,1,0:T(2,128)(2,1)} %reshape.522), calls=%async_computation.3 | async-start | bytes 589824 | tf_op jit(solution)/shard_map/all_to_all | solution.py:93
  949.8 17.0 %copy-start.18 = (bf16[1,2,64,1152]{3,2,1,0:T(8,128)(2,1)S(1)}, bf16[1,2,64,1152]{3,2,1,0:T(8,128)(2,1)}, u32[]{:S(2)}) copy-start(bf16[1,2,64,1152]{3,2,1,0:T(8,128)(2,1)} %param.10) | copy-start | bytes 884740
  960.3 16.5 %all-to-all-start.1 = ((bf16[64,2,1152]{2,1,0:T(2,128)(2,1)}), bf16[64,2,1152]{2,1,0:T(2,128)(2,1)S(1)}, u32[]{:S(2)}, u32[]{:S(2)}) async-start(bf16[64,2,1152]{2,1,0:T(2,128)(2,1)} %reshape.520), calls=%async_computation.1 | async-start | bytes 589824 | tf_op jit(solution)/shard_map/all_to_all | solution.py:79
  966.8 11.0 copy-start.14
  966.8 10.8 copy-start.19
  977.8 128.1 %copy-start.3 = (bf16[1,2,64,1152]{3,2,1,0:T(8,128)(2,1)}, bf16[1,2,64,1152]{3,2,1,0:T(8,128)(2,1)S(1)}, u32[]{:S(2)}) copy-start(bf16[1,2,64,1152]{3,2,1,0:T(8,128)(2,1)S(1)} %get-tuple-element.14) | copy-start | bytes 884740
  1101.8 3.6 copy-start
  1104.8 1.1 copy-start.11
  1104.8 1.1 copy-start.13
Sparse Core Ops, SparseCore 0:
  142.2 59.9 all-gather.10
  270.9 110.1 all-gather.8
  678.4 83.5 reduce-scatter.3
  805.2 108.5 all-gather.14
  936.1 157.3 all-gather.12
where the time goes:
time: 1110 us
  blocking collectives  803 us (72%)
  waiting for transfers between devices  222 us (20%)
  matrix products  23.2 us (2%)
  local copies, waits for them, and re-layouts  19.8 us (2%)
  starting transfers between devices  19.7 us (2%)
  between operations  15.2 us (1%)
    unnamed x1, blocking collectives  287 us
    all_gather x1, blocking collectives, body(): lax.all_gather(w_out_time, 'seq', axis=0, tiled=True)  134 us
    all_gather x1, blocking collectives, body(): lax.all_gather(w_qkv_space, 'seq', axis=0, tiled=True)  130 us
    all_gather x1, blocking collectives, body(): lax.all_gather(w_qkv_time, 'seq', axis=0, tiled=True)  127 us
    all_gather x1, blocking collectives, body(): lax.all_gather(w_out_space, 'seq', axis=0, tiled=True)  126 us
    all_gather x1, waiting for transfers between devices, body(): lax.all_gather(part_a, 'dp', axis=1, tiled=True)  115 us
    all_gather x1, waiting for transfers between devices, body(): lax.all_gather(part_c, 'dp', axis=1, tiled=True)  75.2 us
  transfers between devices with their start and end apart: 9, of which 6 were waited for; matrix products, arithmetic and copies ran while one was open for 3% of the time, Pallas kernels for 0%

commit v1 on v0

--- a/solution.py
+++ b/solution.py
@@ -15,6 +15,21 @@
         return part.astype(jnp.bfloat16) if part.dtype == jnp.float32 else part
 
     return jax.tree.map(short, shard)
+
+
+def gather_weight(shard):
+    rows, cols = shard.shape
+    blocks = lax.all_gather(shard, ("dp", "seq"), axis=0, tiled=False)
+    dp, seq = lax.axis_size("dp"), lax.axis_size("seq")
+    blocks = blocks.reshape(dp, seq, rows, cols).transpose(1, 2, 0, 3)
+    return blocks.reshape(seq * rows, dp * cols)
+
+
+def scatter_grad(partial, dp, seq):
+    rows, cols = partial.shape
+    blocks = partial.reshape(seq, rows // seq, dp, cols // dp).transpose(2, 0, 1, 3)
+    blocks = blocks.reshape(dp * seq * (rows // seq), cols // dp)
+    return lax.psum_scatter(blocks, ("dp", "seq"), scatter_dimension=0, tiled=True)
 
 
 def normalize(values):
@@ -50,17 +65,8 @@
 def body(
     y_first, y_second, grad_first, grad_second, w_qkv_space, w_out_space, w_qkv_time, w_out_time
 ):
-    part_a, part_b, part_c, part_d = (
-        lax.all_gather(w_qkv_space, "seq", axis=0, tiled=True),
-        lax.all_gather(w_out_space, "seq", axis=0, tiled=True),
-        lax.all_gather(w_qkv_time, "seq", axis=0, tiled=True),
-        lax.all_gather(w_out_time, "seq", axis=0, tiled=True),
-    )
     space_qkv, space_proj, time_qkv, time_proj = (
-        lax.all_gather(part_a, "dp", axis=1, tiled=True),
-        lax.all_gather(part_b, "dp", axis=1, tiled=True),
-        lax.all_gather(part_c, "dp", axis=1, tiled=True),
-        lax.all_gather(part_d, "dp", axis=1, tiled=True),
+        gather_weight(w) for w in (w_qkv_space, w_out_space, w_qkv_time, w_out_time)
     )
     frame_count = y_first.shape[1]
     tokens = y_first.shape[2]
@@ -106,10 +112,7 @@
         (((0,), (0,)), ((), ())),
         preferred_element_type=jnp.float32,
     )
-    row_share = lax.psum_scatter(partial_grad, "seq", scatter_dimension=0, tiled=True)
-    grad_share = lax.psum_scatter(
-        row_share.astype(jnp.bfloat16), "dp", scatter_dimension=1, tiled=True
-    ).astype(jnp.float32)
+    grad_share = scatter_grad(partial_grad, lax.axis_size("dp"), lax.axis_size("seq"))
     return (first_in, second_in, first_grad, second_grad, grad_share)
 
 

time: 1110 us -> 6090 us (5.49)
  waiting for transfers between devices: 222 us -> 5900 us
  blocking collectives: 803 us -> 0 us
  local copies, waits for them, and re-layouts: 19.8 us -> 90.5 us
    all_gather x4, waiting for transfers between devices: 191 us -> 5610 us  [gather_weight(): blocks = lax.all_gather(shard, ('dp', 'seq'), axis=0, tiled=False)]
    all_gather x4 -> x0, blocking collectives: 516 us -> none  [the longest x1 134 us: body(): lax.all_gather(w_out_time, 'seq', axis=0, tiled=True)]
    unnamed x1 -> x0, blocking collectives: 287 us -> none
    unnamed x6, waiting for transfers between devices: 0.08 us -> 265 us
    reshape x0 -> x9, local copies, waits for them, and re-layouts: none -> 66.1 us  [the longest x4 32.4 us: gather_weight(): blocks = blocks.reshape(dp, seq, rows, cols).transpose(1, 2, 0, 3)]
  transfers between devices with their start and end apart: 9 -> 9, of which waited for: 6 -> 8; matrix products, arithmetic and copies ran while one was open for 3% -> 2% of each run, Pallas kernels for 0% -> 0%
where the time goes in v1:
time: 6090 us; the launch traced here: 6080 us
  waiting for transfers between devices  5900 us (97%)
  local copies, waits for them, and re-layouts  90.5 us (1%)
    all_gather x4, waiting for transfers between devices, gather_weight(): blocks = lax.all_gather(shard, ('dp', 'seq'), axis=0, tiled=False)  5610 us
    unnamed x6, waiting for transfers between devices  265 us
  transfers between devices with their start and end apart: 9, of which 8 were waited for; matrix products, arithmetic and copies ran while one was open for 2% of the time, Pallas kernels for 0%

profile of v1, /device:TPU:1, one launch (start us, length us, event | category | flops | bytes accessed | tf_op | source)
XLA Modules:
  0.0 6077.9 jit_solution(9650900695592990234)
XLA Ops:
  7.9 0.7 all-gather.13.cloned.1.call-update
  8.7 0.7 all-gather.19.cloned.1.call-update
  10.0 2.0 copy.57
  11.9 12.9 all-to-all-start
  24.9 2.0 copy.73
  26.8 10.2 all-to-all-done
  37.1 5.8 all-to-all-start.2
  43.5 0.9 reshape.578
  45.1 9.4 all-to-all-done.2
  54.7 1.3 multiply_convert_fusion
  56.0 1388.1 %all-gather.15.cloned.1.call-done = bf16[512,9,144]{2,1,0:T(8,128)(2,1)} async-done(((bf16[1,9,144]{2,1,0:T(8,128)(2,1)}), bf16[512,9,144]{2,1,0:T(8,128)(2,1)}) %all-gather.15.cloned.1.call-update) | async-done | bytes 1327120 | tf_op jit(solution)/shard_map/all_gather | solution.py:22
  1444.0 6.2 copy.128
  1450.2 4.0 reshape.559
  1454.7 1423.8 %all-gather.13.cloned.1.call-done = bf16[512,18,216]{2,1,0:T(8,128)(2,1)} async-done(((bf16[1,18,216]{2,1,0:T(8,128)(2,1)}), bf16[512,18,216]{2,1,0:T(8,128)(2,1)}) %all-gather.13.cloned.1.call-update) | async-done | bytes 3981328 | tf_op jit(solution)/shard_map/all_gather | solution.py:22
  2878.5 10.0 copy.126
  2888.6 9.2 reshape.552
  2897.8 3.8 convolution_convert_fusion.5
  2903.8 1.5 multiply_reduce_fusion
  2906.5 2.4 reduce.28
  2908.9 0.8 reshape.615
  2909.7 12.8 all-to-all-start.3
  2923.7 2.4 reduce.29
  2926.1 0.8 reshape.613
  2926.9 8.9 all-to-all-done.3
  2935.8 5.1 all-to-all-start.1
  2941.1 1371.0 %all-gather.19.cloned.1.call-done = bf16[512,9,144]{2,1,0:T(8,128)(2,1)} async-done(((bf16[1,9,144]{2,1,0:T(8,128)(2,1)}), bf16[512,9,144]{2,1,0:T(8,128)(2,1)}) %all-gather.19.cloned.1.call-update) | async-done | bytes 1327120 | tf_op jit(solution)/shard_map/all_gather | solution.py:22
  4312.1 6.1 copy.127
  4318.3 4.3 reshape.569
  4322.6 1423.6 %all-gather.17.cloned.1.call-done = bf16[512,18,216]{2,1,0:T(8,128)(2,1)} async-done(((bf16[1,18,216]{2,1,0:T(8,128)(2,1)}), bf16[512,18,216]{2,1,0:T(8,128)(2,1)}) %all-gather.17.cloned.1.call-update) | async-done | bytes 3981328 | tf_op jit(solution)/shard_map/all_gather | solution.py:22
  5746.1 10.1 copy.125
  5756.2 9.0 reshape.562
  5765.3 0.8 convolution_bitcast_fusion
  5766.1 6.1 copy.86
  5772.3 7.1 reshape.577
  5779.6 1.4 convert.18
  5782.8 3.8 convolution_convert_fusion.3
  5787.0 1.3 fusion.61
  5788.4 1.9 copy.100
  5791.7 1.2 fusion.5
  5793.1 0.9 reshape.567
  5794.0 1.3 convolution_convert_fusion.2
  5795.3 2.0 fusion.20
  5798.3 1.3 convert_reduce_fusion
  5799.6 0.9 fusion.58
  5802.6 3.6 fusion
  5806.4 0.9 add_convert_fusion
  5807.3 262.5 %all-reduce.9.cloned.1.call-done = f32[4608,144]{1,0:T(8,128)} async-done(((f32[4608,144]{1,0:T(8,128)}), f32[4608,144]{1,0:T(8,128)}) %all-reduce.9.cloned.1.call-update) | async-done | bytes 2654224
  6069.8 1.3 constant_dynamic-slice_fusion
  (95 shorter events, 15.1 us)
Async XLA Ops:
  7.2 1436.9 %all-gather.15.cloned.1.call-start = ((), (), s32[]{:S(2)}) async-start(), calls=%async_computation.5 | async-start | bytes 4202496 | tf_op jit(solution)/shard_map/all_gather | solution.py:22
  7.9 2870.6 %all-gather.13.cloned.1.call-start = ((), (), s32[]{:S(2)}) async-start(), calls=%async_computation.4 | async-start | bytes 6303744 | tf_op jit(solution)/shard_map/all_gather | solution.py:22
  8.6 4303.5 %all-gather.19.cloned.1.call-start = ((), (), s32[]{:S(2)}) async-start(), calls=%async_computation.7 | async-start | bytes 4202496 | tf_op jit(solution)/shard_map/all_gather | solution.py:22
  9.4 5736.7 %all-gather.17.cloned.1.call-start = ((), (), s32[]{:S(2)}) async-start(), calls=%async_computation.6 | async-start | bytes 6303744 | tf_op jit(solution)/shard_map/all_gather | solution.py:22
  11.9 25.1 all-to-all-start
  37.1 17.5 all-to-all-start.2
  2888.6 9.3 copy-start.3
  2901.6 2.2 copy-start
  2909.7 26.1 all-to-all-start.3
  2935.8 2845.2 %all-to-all-start.1 = ((bf16[64,2,1152]{2,1,0:T(2,128)(2,1)}), bf16[64,2,1152]{2,1,0:T(2,128)(2,1)S(1)}, u32[]{:S(2)}, u32[]{:S(2)}) async-start(bf16[64,2,1152]{2,1,0:T(2,128)(2,1)} %reshape.613), calls=%async_computation.1 | async-start | bytes 589824 | tf_op jit(solution)/shard_map/all_to_all | solution.py:85
  2940.9 3129.0 %all-reduce.9.cloned.1.call-start = ((), (), s32[]{:S(2)}) async-start(), calls=%async_computation.8 | async-start | bytes 9437184
  5779.3 2.8 copy-start.6
  5782.3 0.6 copy-start.13
  5782.3 24.1 copy-start.1
  5782.3 0.6 copy-start.11
  5788.4 6.9 copy-start.2
  5790.9 0.7 copy-start.7
  5791.1 1.9 copy-start.9
  5797.3 3.8 copy-start.4
  5797.8 3.3 copy-start.8
  5797.8 3.3 copy-start.10
  5801.5 4.8 copy-start.14
  5801.5 4.9 copy-start.5
  5801.5 4.9 copy-start.12
Sparse Core Ops, SparseCore 0:
  10.2 1433.7 all-gather.14
  1446.3 1432.2 all-gather.12
  2880.8 1431.3 all-gather.18
  4314.2 1431.8 all-gather.16
  5779.5 290.3 all-reduce.8

commit v2 on v1

--- a/solution.py
+++ b/solution.py
@@ -3,10 +3,27 @@
 import jax
 import jax.numpy as jnp
 from jax import lax
-from jax.sharding import PartitionSpec as P
+from jax.sharding import Mesh, PartitionSpec as P
 
 HEADS = 8
 HD = 72
+
+DP = ("zh", "core")
+SEQ = ("x", "zl", "y")
+
+
+def gather_weight(shard):
+    for axis, dim in (("core", 1), ("zh", 1), ("y", 0), ("zl", 0), ("x", 0)):
+        shard = lax.all_gather(shard, axis, axis=dim, tiled=True)
+    return shard
+
+
+def scatter_grad(partial):
+    rows, cols = partial.shape
+    dp, seq = lax.axis_size(DP), lax.axis_size(SEQ)
+    blocks = partial.reshape(seq, rows // seq, dp, cols // dp).transpose(2, 0, 1, 3)
+    blocks = blocks.reshape(dp * seq, rows // seq, cols // dp)
+    return lax.all_to_all(blocks, DP + SEQ, 0, 0, tiled=True).sum(0)
 
 
 def for_sending(shard):
@@ -15,21 +32,6 @@
         return part.astype(jnp.bfloat16) if part.dtype == jnp.float32 else part
 
     return jax.tree.map(short, shard)
-
-
-def gather_weight(shard):
-    rows, cols = shard.shape
-    blocks = lax.all_gather(shard, ("dp", "seq"), axis=0, tiled=False)
-    dp, seq = lax.axis_size("dp"), lax.axis_size("seq")
-    blocks = blocks.reshape(dp, seq, rows, cols).transpose(1, 2, 0, 3)
-    return blocks.reshape(seq * rows, dp * cols)
-
-
-def scatter_grad(partial, dp, seq):
-    rows, cols = partial.shape
-    blocks = partial.reshape(seq, rows // seq, dp, cols // dp).transpose(2, 0, 1, 3)
-    blocks = blocks.reshape(dp * seq * (rows // seq), cols // dp)
-    return lax.psum_scatter(blocks, ("dp", "seq"), scatter_dimension=0, tiled=True)
 
 
 def normalize(values):
@@ -78,11 +80,11 @@
     def space_fn(inputs):
         return attend(inputs, space_qkv, space_proj)[0]
 
-    first_patch = lax.all_to_all(y_first, "seq", split_axis=2, concat_axis=1, tiled=True)
+    first_patch = lax.all_to_all(y_first, SEQ, split_axis=2, concat_axis=1, tiled=True)
     time_out, time_vjp, time_mixed = jax.vjp(time_fn, first_patch, has_aux=True)
     time_frames = jax.tree.map(
         lambda part, own: part.astype(own.dtype),
-        lax.all_to_all(for_sending(time_out), "seq", split_axis=1, concat_axis=2, tiled=True),
+        lax.all_to_all(for_sending(time_out), SEQ, split_axis=1, concat_axis=2, tiled=True),
         time_out,
     )
     second_in = (y_second.astype(jnp.float32) - time_frames.astype(jnp.float32)).astype(
@@ -92,11 +94,11 @@
     first_in = (
         y_first.astype(jnp.float32) - space_out.reshape(y_first.shape).astype(jnp.float32)
     ).astype(jnp.bfloat16)
-    cot_patch = lax.all_to_all(grad_second, "seq", split_axis=2, concat_axis=1, tiled=True)
+    cot_patch = lax.all_to_all(grad_second, SEQ, split_axis=2, concat_axis=1, tiled=True)
     back_patch = time_vjp(cot_patch)[0]
     back_frames = jax.tree.map(
         lambda part, own: part.astype(own.dtype),
-        lax.all_to_all(for_sending(back_patch), "seq", split_axis=1, concat_axis=2, tiled=True),
+        lax.all_to_all(for_sending(back_patch), SEQ, split_axis=1, concat_axis=2, tiled=True),
         back_patch,
     )
     first_grad = (grad_first.astype(jnp.float32) + back_frames.astype(jnp.float32)).astype(
@@ -112,31 +114,34 @@
         (((0,), (0,)), ((), ())),
         preferred_element_type=jnp.float32,
     )
-    grad_share = scatter_grad(partial_grad, lax.axis_size("dp"), lax.axis_size("seq"))
+    grad_share = scatter_grad(partial_grad)
     return (first_in, second_in, first_grad, second_grad, grad_share)
 
 
 def solution(mesh):
     placed = (
-        P("dp", "seq", None, None),
-        P("dp", "seq", None, None),
-        P("dp", "seq", None, None),
-        P("dp", "seq", None, None),
-        P("seq", "dp"),
-        P("seq", "dp"),
-        P("seq", "dp"),
-        P("seq", "dp"),
+        P(DP, SEQ, None, None),
+        P(DP, SEQ, None, None),
+        P(DP, SEQ, None, None),
+        P(DP, SEQ, None, None),
+        P(SEQ, DP),
+        P(SEQ, DP),
+        P(SEQ, DP),
+        P(SEQ, DP),
     )
+    dp, seq = mesh.devices.shape
+    split = (dp // 2, 2, seq // 16, 2, 8)
+    full = Mesh(mesh.devices.reshape(split), DP + SEQ)
     return jax.shard_map(
         body,
-        mesh=mesh,
+        mesh=full,
         in_specs=placed,
         out_specs=(
-            P("dp", "seq", None, None),
-            P("dp", "seq", None, None),
-            P("dp", "seq", None, None),
-            P("dp", "seq", None, None),
-            P("seq", "dp"),
+            P(DP, SEQ, None, None),
+            P(DP, SEQ, None, None),
+            P(DP, SEQ, None, None),
+            P(DP, SEQ, None, None),
+            P(SEQ, DP),
         ),
         check_vma=False,
     )

time: 6090 us -> 429 us (0.07)
  waiting for transfers between devices: 5900 us -> 40.8 us
  blocking collectives: 0 us -> 199 us
    all_gather x4, waiting for transfers between devices: 5610 us -> 0.06 us  [gather_weight(): shard = lax.all_gather(shard, axis, axis=dim, tiled=True)]
    unnamed x6 -> x4, waiting for transfers between devices: 265 us -> 0.07 us
    all_gather x0 -> x16, blocking collectives: none -> 199 us  [gather_weight(): shard = lax.all_gather(shard, axis, axis=dim, tiled=True)]
  transfers between devices with their start and end apart: 9 -> 9, of which waited for: 8 -> 3; matrix products, arithmetic and copies ran while one was open for 2% -> 21% of each run, Pallas kernels for 0% -> 0%
where the time goes in v2:
time: 429 us; the launch traced here: 423 us
  blocking collectives  199 us (46%)
  local copies, waits for them, and re-layouts  56.2 us (13%)
  starting transfers between devices  56.2 us (13%)
  waiting for transfers between devices  40.8 us (10%)
  other arithmetic  28.1 us (7%)
  matrix products  27.8 us (6%)
  between operations  14.7 us (3%)
    all_gather x16, blocking collectives, gather_weight(): shard = lax.all_gather(shard, axis, axis=dim, tiled=True)  199 us
    unnamed x73, local copies, waits for them, and re-layouts  32.4 us
    all_to_all x1, waiting for transfers between devices, scatter_grad(): return lax.all_to_all(blocks, DP + SEQ, 0, 0, tiled=True).sum(0)  27.3 us
    all_to_all x1, starting transfers between devices, scatter_grad(): return lax.all_to_all(blocks, DP + SEQ, 0, 0, tiled=True).sum(0)  24.3 us
    dot_general x4, matrix products, attend(): jnp.dot(normed, w_qkv, preferred_element_type=jnp.float32)  16 us
    all_to_all x1, other arithmetic, scatter_grad(): return lax.all_to_all(blocks, DP + SEQ, 0, 0, tiled=True).sum(0)  10.1 us
    all_to_all x1, starting transfers between devices, body(): lax.all_to_all(grad_second, SEQ, split_axis=2, concat_axis=1, tiled=True)  9.88 us
    all_to_all x1, waiting for transfers between devices, body(): lax.all_to_all(grad_second, SEQ, split_axis=2, concat_axis=1, tiled=True)  9.88 us
  transfers between devices with their start and end apart: 9, of which 3 were waited for; matrix products, arithmetic and copies ran while one was open for 21% of the time, Pallas kernels for 0%

profile of v2, /device:TPU:1, one launch (start us, length us, event | category | flops | bytes accessed | tf_op | source)
XLA Modules:
  0.0 423.2 jit_solution(16716290496637654876)
XLA Ops:
  7.2 8.5 %all-gather.3 = bf16[2,144,9]{1,2,0:T(8,128)(2,1)S(1)} all-gather(bf16[1,144,9]{1,2,0:T(8,128)(2,1)} %bitcast.262), channel_id=1, replica_groups=mesh['zh'=4,'core'=2,'x'=4,'zl'=2,'y'=8] {'core'}, dimensions={0}, use_global_device_ids=true | all-gather | bytes 7776 | tf_op jit(solution)/shard_map/all_gather | solution.py:17
  15.9 11.2 %all-gather.4 = bf16[4,288,9]{1,2,0:T(8,128)(2,1)S(1)} all-gather(bf16[1,288,9]{1,2,0:T(8,128)(2,1)S(1)} %reshape.523), channel_id=1, replica_groups=mesh['zh'=4,'core'=2,'x'=4,'zl'=2,'y'=8] {'zh'}, dimensions={0}, use_global_device_ids=true | all-gather | bytes 25920 | tf_op jit(solution)/shard_map/all_gather | solution.py:17
  27.1 20.5 %all-gather.5 = bf16[8,9,1152]{2,1,0:T(8,128)(2,1)S(1)} all-gather(bf16[1,9,1152]{2,1,0:T(8,128)(2,1)S(1)} %bitcast.258), channel_id=1, replica_groups=mesh['zh'=4,'core'=2,'x'=4,'zl'=2,'y'=8] {'y'}, dimensions={0}, use_global_device_ids=true | all-gather | bytes 186624 | tf_op jit(solution)/shard_map/all_gather | solution.py:17
  47.7 5.2 %all_gather.68 = bf16[144,1152]{1,0:T(8,128)(2,1)} all-gather(bf16[72,1152]{1,0:T(8,128)(2,1)S(1)} %reshape.526), channel_id=1, replica_groups=mesh['zh'=4,'core'=2,'x'=4,'zl'=2,'y'=8] {'zl'}, dimensions={0}, use_global_device_ids=true | all-gather | bytes 497664 | tf_op jit(solution)/shard_map/all_gather | solution.py:17
  52.9 11.6 %all-gather = bf16[2,216,18]{1,2,0:T(8,128)(2,1)S(1)} all-gather(bf16[1,216,18]{1,2,0:T(8,128)(2,1)} %bitcast.260), channel_id=1, replica_groups=mesh['zh'=4,'core'=2,'x'=4,'zl'=2,'y'=8] {'core'}, dimensions={0}, use_global_device_ids=true | all-gather | bytes 23328 | tf_op jit(solution)/shard_map/all_gather | solution.py:17
  64.6 11.2 %all-gather.1 = bf16[4,432,18]{1,2,0:T(8,128)(2,1)S(1)} all-gather(bf16[1,432,18]{1,2,0:T(8,128)(2,1)S(1)} %reshape.517), channel_id=1, replica_groups=mesh['zh'=4,'core'=2,'x'=4,'zl'=2,'y'=8] {'zh'}, dimensions={0}, use_global_device_ids=true | all-gather | bytes 77760 | tf_op jit(solution)/shard_map/all_gather | solution.py:17
  76.0 21.6 %all-gather.2 = bf16[8,18,1728]{2,1,0:T(8,128)(2,1)S(1)} all-gather(bf16[1,18,1728]{2,1,0:T(8,128)(2,1)S(1)} %bitcast.254), channel_id=1, replica_groups=mesh['zh'=4,'core'=2,'x'=4,'zl'=2,'y'=8] {'y'}, dimensions={0}, use_global_device_ids=true | all-gather | bytes 559872 | tf_op jit(solution)/shard_map/all_gather | solution.py:17
  98.0 8.8 %all_gather.63 = bf16[288,1728]{1,0:T(8,128)(2,1)} all-gather(bf16[144,1728]{1,0:T(8,128)(2,1)S(1)} %reshape.520), channel_id=1, replica_groups=mesh['zh'=4,'core'=2,'x'=4,'zl'=2,'y'=8] {'zl'}, dimensions={0}, use_global_device_ids=true | all-gather | bytes 1492992 | tf_op jit(solution)/shard_map/all_gather | solution.py:17
  106.9 9.9 %all-gather.6 = bf16[2,216,18]{1,2,0:T(8,128)(2,1)S(1)} all-gather(bf16[1,216,18]{1,2,0:T(8,128)(2,1)S(1)} %bitcast.261), channel_id=1, replica_groups=mesh['zh'=4,'core'=2,'x'=4,'zl'=2,'y'=8] {'core'}, dimensions={0}, use_global_device_ids=true | all-gather | bytes 23328 | tf_op jit(solution)/shard_map/all_gather | solution.py:17
  117.0 11.2 %all-gather.7 = bf16[4,432,18]{1,2,0:T(8,128)(2,1)S(1)} all-gather(bf16[1,432,18]{1,2,0:T(8,128)(2,1)S(1)} %reshape.529), channel_id=1, replica_groups=mesh['zh'=4,'core'=2,'x'=4,'zl'=2,'y'=8] {'zh'}, dimensions={0}, use_global_device_ids=true | all-gather | bytes 77760 | tf_op jit(solution)/shard_map/all_gather | solution.py:17
  128.3 22.1 %all-gather.8 = bf16[8,18,1728]{2,1,0:T(8,128)(2,1)S(1)} all-gather(bf16[1,18,1728]{2,1,0:T(8,128)(2,1)S(1)} %bitcast.255), channel_id=1, replica_groups=mesh['zh'=4,'core'=2,'x'=4,'zl'=2,'y'=8] {'y'}, dimensions={0}, use_global_device_ids=true | all-gather | bytes 559872 | tf_op jit(solution)/shard_map/all_gather | solution.py:17
  150.7 9.0 %all_gather.73 = bf16[288,1728]{1,0:T(8,128)(2,1)} all-gather(bf16[144,1728]{1,0:T(8,128)(2,1)S(1)} %reshape.532), channel_id=1, replica_groups=mesh['zh'=4,'core'=2,'x'=4,'zl'=2,'y'=8] {'zl'}, dimensions={0}, use_global_device_ids=true | all-gather | bytes 1492992 | tf_op jit(solution)/shard_map/all_gather | solution.py:17
  160.7 9.7 %all-to-all-start = ((bf16[1,2,64,1152]{3,1,0,2:T(2,128)(2,1)}), bf16[1,2,64,1152]{3,1,0,2:T(2,128)(2,1)S(1)}, u32[]{:S(2)}, u32[]{:S(2)}) async-start(bf16[1,2,64,1152]{3,1,0,2:T(2,128)(2,1)} %copy.189), calls=%async_computation | async-start | bytes 589824 | tf_op jit(solution)/shard_map/all_to_all | solution.py:83
  170.5 9.6 %all-gather.9 = bf16[2,144,9]{1,2,0:T(8,128)(2,1)S(1)} all-gather(bf16[1,144,9]{1,2,0:T(8,128)(2,1)S(1)} %bitcast.263), channel_id=1, replica_groups=mesh['zh'=4,'core'=2,'x'=4,'zl'=2,'y'=8] {'core'}, dimensions={0}, use_global_device_ids=true | all-gather | bytes 7776 | tf_op jit(solution)/shard_map/all_gather | solution.py:17
  180.2 11.6 %all-gather.10 = bf16[4,288,9]{1,2,0:T(8,128)(2,1)S(1)} all-gather(bf16[1,288,9]{1,2,0:T(8,128)(2,1)S(1)} %reshape.535), channel_id=1, replica_groups=mesh['zh'=4,'core'=2,'x'=4,'zl'=2,'y'=8] {'zh'}, dimensions={0}, use_global_device_ids=true | all-gather | bytes 25920 | tf_op jit(solution)/shard_map/all_gather | solution.py:17
  191.9 22.2 %all-gather.11 = bf16[8,9,1152]{2,1,0:T(8,128)(2,1)S(1)} all-gather(bf16[1,9,1152]{2,1,0:T(8,128)(2,1)S(1)} %bitcast.259), channel_id=1, replica_groups=mesh['zh'=4,'core'=2,'x'=4,'zl'=2,'y'=8] {'y'}, dimensions={0}, use_global_device_ids=true | all-gather | bytes 186624 | tf_op jit(solution)/shard_map/all_gather | solution.py:17
  214.2 5.3 %all_gather.78 = bf16[144,1152]{1,0:T(8,128)(2,1)} all-gather(bf16[72,1152]{1,0:T(8,128)(2,1)S(1)} %reshape.538), channel_id=1, replica_groups=mesh['zh'=4,'core'=2,'x'=4,'zl'=2,'y'=8] {'zl'}, dimensions={0}, use_global_device_ids=true | all-gather | bytes 497664 | tf_op jit(solution)/shard_map/all_gather | solution.py:17
  220.5 9.9 %all-to-all-start.2 = ((bf16[1,2,64,1152]{3,1,0,2:T(2,128)(2,1)}), bf16[1,2,64,1152]{3,1,0,2:T(2,128)(2,1)S(1)}, u32[]{:S(2)}, u32[]{:S(2)}) async-start(bf16[1,2,64,1152]{3,1,0,2:T(2,128)(2,1)} %copy.209), calls=%async_computation.2 | async-start | bytes 589824 | tf_op jit(solution)/shard_map/all_to_all | solution.py:97
  231.7 9.9 %all-to-all-done.2 = bf16[1,2,64,1152]{3,1,0,2:T(2,128)(2,1)S(1)} async-done(((bf16[1,2,64,1152]{3,1,0,2:T(2,128)(2,1)}), bf16[1,2,64,1152]{3,1,0,2:T(2,128)(2,1)S(1)}, u32[]{:S(2)}, u32[]{:S(2)}) %all-to-all-start.2) | async-done | bytes 294944 | tf_op jit(solution)/shard_map/all_to_all | solution.py:97
  242.0 1.8 convolution_convert_fusion.17
  243.8 3.9 convolution_convert_fusion.5
  251.3 2.4 reduce.28
  254.5 4.8 %all-to-all-start.1 = ((bf16[64,2,1152]{2,1,0:T(2,128)(2,1)}), bf16[64,2,1152]{2,1,0:T(2,128)(2,1)S(1)}, u32[]{:S(2)}, u32[]{:S(2)}) async-start(bf16[64,2,1152]{2,1,0:T(2,128)(2,1)} %reshape.546), calls=%async_computation.1 | async-start | bytes 589824 | tf_op jit(solution)/shard_map/all_to_all | solution.py:87
  259.4 3.7 multiply_reduce_fusion
  263.7 2.4 reduce.29
  267.0 3.5 all-to-all-done.1
  270.6 7.3 %all-to-all-start.3 = ((bf16[64,2,1152]{2,1,0:T(2,128)(2,1)}), bf16[64,2,1152]{2,1,0:T(2,128)(2,1)S(1)}, u32[]{:S(2)}, u32[]{:S(2)}) async-start(bf16[64,2,1152]{2,1,0:T(2,128)(2,1)} %reshape.548), calls=%async_computation.3 | async-start | bytes 589824 | tf_op jit(solution)/shard_map/all_to_all | solution.py:101
  278.7 6.2 %copy.222 = f32[512,9,144]{2,1,0:T(8,128)} copy(f32[512,9,144]{2,0,1:T(8,128)S(1)} %bitcast.231) | data formatting | bytes 5308416 | tf_op jit(solution)/shard_map/reshape | solution.py:25
  284.9 9.9 %reshape.550 = f32[512,1,1296]{2,1,0:T(1,128)} reshape(f32[512,9,144]{2,1,0:T(8,128)} %copy.222) | data formatting | bytes 5308416
  296.6 24.3 %all-to-all-start.4 = ((f32[512,1,1296]{2,1,0:T(1,128)}), f32[512,1,1296]{2,1,0:T(1,128)S(1)}, u32[]{:S(2)}, u32[]{:S(2)}) async-start(f32[512,1,1296]{2,1,0:T(1,128)} %reshape.550), calls=%async_computation.4 | async-start | bytes 5767168 | tf_op jit(solution)/shard_map/all_to_all | solution.py:26
  321.1 4.6 %convolution_convert_fusion.3 = bf16[128,1728]{0,1:T(8,128)(2,1)} fusion(bf16[128,1152]{1,0:T(8,128)(2,1)S(1)} %fusion.20, bf16[1152,1728]{1,0:T(8,128)(2,1)} %all-gather.21.cloned.1.call-done), kind=kOutput, calls=%fused_computation.5 | convolution fusion | flops 509829120 | bytes 4718592 | tf_op jit(solution)/shard_map/jvp()/dot_general | solution.py:46
  325.7 2.9 reshape.545
  328.6 2.5 fusion.59
  331.1 1.8 copy.234
  338.7 1.9 reshape.495
  340.6 3.0 reshape.549
  343.6 1.7 convert.16
  345.3 1.7 fusion.15
  347.0 1.9 convolution_convert_fusion.16
  349.8 1.9 reshape.500
  352.5 1.4 convert_reduce_fusion
  355.8 1.4 copy.219
  357.3 2.6 reshape.502
  359.9 3.8 fusion
  365.5 27.3 %all-to-all-done.4 = f32[512,1,1296]{2,1,0:T(1,128)S(1)} async-done(((f32[512,1,1296]{2,1,0:T(1,128)}), f32[512,1,1296]{2,1,0:T(1,128)S(1)}, u32[]{:S(2)}, u32[]{:S(2)}) %all-to-all-start.4) | async-done | bytes 2654240 | tf_op jit(solution)/shard_map/all_to_all | solution.py:26
  393.3 10.1 %reduce.30 = f32[512,1296]{1,0:T(8,128)} reduce(f32[512,1,1296]{2,1,0:T(1,128)S(1)} %all-to-all-done.4, f32[]{:T(128)} %broadcast.223), dimensions={1}, to_apply=%all_to_all.20.reduce_sub_computation | reduce | bytes 5308420 | tf_op jit(solution)/shard_map/all_to_all | solution.py:26
  403.4 8.5 %reshape.551 = f32[512,9,144]{2,1,0:T(8,128)} reshape(f32[512,1296]{1,0:T(8,128)} %reduce.30) | data formatting | bytes 5308416
  411.9 4.6 %reduce_sum.153 = f32[9,144]{1,0:T(8,128)} reduce(f32[512,9,144]{2,1,0:T(8,128)} %reshape.551, f32[]{:T(128)} %constant.10.clone.1), dimensions={0}, to_apply=%region_14.0 | reduce | flops 662256 | bytes 2659396 | tf_op jit(solution)/shard_map/reduce_sum | solution.py:26
  (142 shorter events, 25.8 us)
Async XLA Ops:
  7.2 99.7 %copy-start.18 = (bf16[18,216]{1,0:T(8,128)(2,1)S(1)}, bf16[18,216]{1,0:T(8,128)(2,1)}, u32[]{:S(2)}) copy-start(bf16[18,216]{1,0:T(8,128)(2,1)} %param.12) | copy-start | bytes 23332
  7.2 234.8 %all-gather.19.cloned.1.call-start = ((), (), s32[]{:S(2)}) async-start(), calls=%async_computation.6 | async-start | bytes 1658880 | tf_op jit(solution)/shard_map/all_gather | solution.py:17
  52.9 190.9 %all-gather.17.cloned.1.call-start = ((), (), s32[]{:S(2)}) async-start(), calls=%async_computation.5 | async-start | bytes 5160960 | tf_op jit(solution)/shard_map/all_gather | solution.py:17
  97.9 61.8 %copy-start.7 = (bf16[1,2,64,1152]{3,2,1,0:T(8,128)(2,1)S(1)}, bf16[1,2,64,1152]{3,2,1,0:T(8,128)(2,1)}, u32[]{:S(2)}) copy-start(bf16[1,2,64,1152]{3,2,1,0:T(8,128)(2,1)} %param.8) | copy-start | bytes 884740
  97.9 72.6 %copy-start.21 = (bf16[9,144]{1,0:T(8,128)(2,1)S(1)}, bf16[9,144]{1,0:T(8,128)(2,1)}, u32[]{:S(2)}) copy-start(bf16[9,144]{1,0:T(8,128)(2,1)} %param.13) | copy-start | bytes 7780
  106.8 112.6 %copy-start.9 = (bf16[1,2,64,1152]{3,2,1,0:T(8,128)(2,1)S(1)}, bf16[1,2,64,1152]{3,2,1,0:T(8,128)(2,1)}, u32[]{:S(2)}) copy-start(bf16[1,2,64,1152]{3,2,1,0:T(8,128)(2,1)} %param.11) | copy-start | bytes 884740
  106.8 214.2 %all-gather.21.cloned.1.call-start = ((), (), s32[]{:S(2)}) async-start(), calls=%async_computation.7 | async-start | bytes 5160960 | tf_op jit(solution)/shard_map/all_gather | solution.py:17
  160.7 59.7 %all-to-all-start = ((bf16[1,2,64,1152]{3,1,0,2:T(2,128)(2,1)}), bf16[1,2,64,1152]{3,1,0,2:T(2,128)(2,1)S(1)}, u32[]{:S(2)}, u32[]{:S(2)}) async-start(bf16[1,2,64,1152]{3,1,0,2:T(2,128)(2,1)} %copy.189), calls=%async_computation | async-start | bytes 589824 | tf_op jit(solution)/shard_map/all_to_all | solution.py:83
  170.5 176.5 %all-gather.23.cloned.1.call-start = ((), (), s32[]{:S(2)}) async-start(), calls=%async_computation.8 | async-start | bytes 1658880 | tf_op jit(solution)/shard_map/all_gather | solution.py:17
  220.5 21.1 %all-to-all-start.2 = ((bf16[1,2,64,1152]{3,1,0,2:T(2,128)(2,1)}), bf16[1,2,64,1152]{3,1,0,2:T(2,128)(2,1)S(1)}, u32[]{:S(2)}, u32[]{:S(2)}) async-start(bf16[1,2,64,1152]{3,1,0,2:T(2,128)(2,1)} %copy.209), calls=%async_computation.2 | async-start | bytes 589824 | tf_op jit(solution)/shard_map/all_to_all | solution.py:97
  247.7 2.1 copy-start.1
  254.5 16.1 %all-to-all-start.1 = ((bf16[64,2,1152]{2,1,0:T(2,128)(2,1)}), bf16[64,2,1152]{2,1,0:T(2,128)(2,1)S(1)}, u32[]{:S(2)}, u32[]{:S(2)}) async-start(bf16[64,2,1152]{2,1,0:T(2,128)(2,1)} %reshape.546), calls=%async_computation.1 | async-start | bytes 589824 | tf_op jit(solution)/shard_map/all_to_all | solution.py:87
  270.6 25.3 %all-to-all-start.3 = ((bf16[64,2,1152]{2,1,0:T(2,128)(2,1)}), bf16[64,2,1152]{2,1,0:T(2,128)(2,1)S(1)}, u32[]{:S(2)}, u32[]{:S(2)}) async-start(bf16[64,2,1152]{2,1,0:T(2,128)(2,1)} %reshape.548), calls=%async_computation.3 | async-start | bytes 589824 | tf_op jit(solution)/shard_map/all_to_all | solution.py:101
  284.9 10.7 %copy-start.12 = (bf16[1,2,64,1152]{3,2,1,0:T(8,128)(2,1)S(1)}, bf16[1,2,64,1152]{3,2,1,0:T(8,128)(2,1)}, u32[]{:S(2)}) copy-start(bf16[1,2,64,1152]{3,2,1,0:T(8,128)(2,1)} %param.9) | copy-start | bytes 884740
  295.8 0.6 copy-start.19
  295.8 29.9 %copy-start.2 = (bf16[1,2,64,1152]{3,2,1,0:T(8,128)(2,1)}, bf16[1,2,64,1152]{3,2,1,0:T(8,128)(2,1)S(1)}, u32[]{:S(2)}) copy-start(bf16[1,2,64,1152]{3,2,1,0:T(8,128)(2,1)S(1)} %get-tuple-element.14) | copy-start | bytes 884740
  295.8 0.6 copy-start.22
  295.9 0.7 copy-start.6
  296.6 96.2 %all-to-all-start.4 = ((f32[512,1,1296]{2,1,0:T(1,128)}), f32[512,1,1296]{2,1,0:T(1,128)S(1)}, u32[]{:S(2)}, u32[]{:S(2)}) async-start(f32[512,1,1296]{2,1,0:T(1,128)} %reshape.550), calls=%async_computation.4 | async-start | bytes 5767168 | tf_op jit(solution)/shard_map/all_to_all | solution.py:26
  335.9 0.6 copy-start.14
  336.5 1.2 copy-start.16
  349.8 5.6 %copy-start.15 = (f32[2,8,64]{2,1,0:T(8,128)S(1)}, f32[2,8,64]{2,1,0:T(8,128)}, u32[]{:S(2)}) copy-start(f32[2,8,64]{2,1,0:T(8,128)} %copy-done.14) | copy-start | bytes 12292
  349.8 5.6 %copy-start.17 = (f32[2,8,64]{2,1,0:T(8,128)S(1)}, f32[2,8,64]{2,1,0:T(8,128)}, u32[]{:S(2)}) copy-start(f32[2,8,64]{2,1,0:T(8,128)} %copy-done.16) | copy-start | bytes 12292
  351.7 3.1 copy-start.4
  351.7 3.4 copy-start.5
  351.7 3.7 copy-start.13
  355.8 8.0 %copy-start.3 = (bf16[1,2,64,1152]{3,2,1,0:T(8,128)(2,1)S(1)}, bf16[1,2,64,1152]{3,2,1,0:T(8,128)(2,1)}, u32[]{:S(2)}) copy-start(bf16[1,2,64,1152]{3,2,1,0:T(8,128)(2,1)} %copy-done.2) | copy-start | bytes 884740
  355.8 8.1 %copy-start.20 = (f32[2,64]{1,0:T(2,128)S(1)}, f32[2,64]{1,0:T(2,128)}, u32[]{:S(2)}) copy-start(f32[2,64]{1,0:T(2,128)} %copy-done.19) | copy-start | bytes 1540
  355.8 8.1 %copy-start.11 = (bf16[128,576]{1,0:T(8,128)(2,1)S(1)}, bf16[128,576]{1,0:T(8,128)(2,1)}, u32[]{:S(2)}) copy-start(bf16[128,576]{1,0:T(8,128)(2,1)} %reshape.495) | copy-start | bytes 442372
  359.9 4.1 copy-start
  359.9 4.5 %copy-start.8 = (bf16[1,2,64,1152]{3,2,1,0:T(8,128)(2,1)S(1)}, bf16[1,2,64,1152]{3,2,1,0:T(8,128)(2,1)}, u32[]{:S(2)}) copy-start(bf16[1,2,64,1152]{3,2,1,0:T(8,128)(2,1)} %param.8) | copy-start | bytes 884740
  359.9 4.5 %copy-start.10 = (bf16[1,2,64,1152]{3,2,1,0:T(8,128)(2,1)S(1)}, bf16[1,2,64,1152]{3,2,1,0:T(8,128)(2,1)}, u32[]{:S(2)}) copy-start(bf16[1,2,64,1152]{3,2,1,0:T(8,128)(2,1)} %param.11) | copy-start | bytes 884740
  359.9 4.5 %copy-start.23 = (f32[2,64]{1,0:T(2,128)S(1)}, f32[2,64]{1,0:T(2,128)}, u32[]{:S(2)}) copy-start(f32[2,64]{1,0:T(2,128)} %copy-done.22) | copy-start | bytes 1540
Sparse Core Ops, SparseCore 0:
  53.0 36.2 all-gather.18
  106.9 58.3 all-gather.16
  167.4 53.7 all-gather.20
  223.2 31.6 all-gather.22

commit v3 on v2

--- a/solution.py
+++ b/solution.py
@@ -12,10 +12,24 @@
 SEQ = ("x", "zl", "y")
 
 
-def gather_weight(shard):
+def gather_weights(qkv_space, out_space, qkv_time, out_time):
+    width = qkv_space.shape[1]
+    pad = ((0, 0), (0, width - out_space.shape[1]))
+    parts = (qkv_space, jnp.pad(out_space, pad), qkv_time, jnp.pad(out_time, pad))
+    block = jnp.concatenate(parts, axis=0)
     for axis, dim in (("core", 1), ("zh", 1), ("y", 0), ("zl", 0), ("x", 0)):
-        shard = lax.all_gather(shard, axis, axis=dim, tiled=True)
-    return shard
+        block = lax.all_gather(block, axis, axis=dim, tiled=True)
+    dp, seq = lax.axis_size(DP), lax.axis_size(SEQ)
+    block = block.reshape(seq, -1, dp * width)
+    outs = []
+    start = 0
+    for shard, part in zip((qkv_space, out_space, qkv_time, out_time), parts):
+        rows, cols = shard.shape
+        piece = block[:, start:start + rows]
+        start += rows
+        piece = piece.reshape(seq * rows, dp, width)[:, :, :cols]
+        outs.append(piece.reshape(seq * rows, dp * cols))
+    return outs
 
 
 def scatter_grad(partial):
@@ -23,7 +37,8 @@
     dp, seq = lax.axis_size(DP), lax.axis_size(SEQ)
     blocks = partial.reshape(seq, rows // seq, dp, cols // dp).transpose(2, 0, 1, 3)
     blocks = blocks.reshape(dp * seq, rows // seq, cols // dp)
-    return lax.all_to_all(blocks, DP + SEQ, 0, 0, tiled=True).sum(0)
+    sent = lax.all_to_all(blocks.astype(jnp.bfloat16), DP + SEQ, 0, 0, tiled=True)
+    return sent.astype(jnp.float32).sum(0)
 
 
 def for_sending(shard):
@@ -67,8 +82,8 @@
 def body(
     y_first, y_second, grad_first, grad_second, w_qkv_space, w_out_space, w_qkv_time, w_out_time
 ):
-    space_qkv, space_proj, time_qkv, time_proj = (
-        gather_weight(w) for w in (w_qkv_space, w_out_space, w_qkv_time, w_out_time)
+    space_qkv, space_proj, time_qkv, time_proj = gather_weights(
+        w_qkv_space, w_out_space, w_qkv_time, w_out_time
     )
     frame_count = y_first.shape[1]
     tokens = y_first.shape[2]

time: 429 us -> 481 us (1.12)
  waiting for transfers between devices: 40.8 us -> 225 us
  blocking collectives: 199 us -> 20.8 us
  local copies, waits for them, and re-layouts: 56.2 us -> 114 us
  other arithmetic: 28.1 us -> 19.9 us
    all_gather x4 -> x3, waiting for transfers between devices: 0.06 us -> 181 us  [gather_weights(): block = lax.all_gather(block, axis, axis=dim, tiled=True)]
    all_gather x16 -> x2, blocking collectives: 199 us -> 20.8 us  [gather_weights(): block = lax.all_gather(block, axis, axis=dim, tiled=True)]
    slice x0 -> x4, local copies, waits for them, and re-layouts: none -> 26.7 us  [the longest x2 18.9 us: gather_weights(): piece = block[:, start:start + rows]]
    reshape x1 -> x3, local copies, waits for them, and re-layouts: 6.19 us -> 30.5 us  [the longest x1 16.2 us: gather_weights(): block = block.reshape(seq, -1, dp * width)]
    another operation x0 -> x2, local copies, waits for them, and re-layouts: none -> 15.4 us  [gather_weights(): outs.append(piece.reshape(seq * rows, dp * cols))]
    all_to_all x1, waiting for transfers between devices: 0.01 us -> 11 us  [body(): lax.all_to_all(y_first, SEQ, split_axis=2, concat_axis=1, tiled=True)]
    all_to_all x1 -> x0, other arithmetic: 10.1 us -> none  [scatter_grad(): return lax.all_to_all(blocks, DP + SEQ, 0, 0, tiled=True).sum(0)]
    all_to_all x1, starting transfers between devices: 24.3 us -> 18.2 us  [scatter_grad(): lax.all_to_all(blocks.astype(jnp.bfloat16), DP + SEQ, 0, 0, tiled=True)]
  transfers between devices with their start and end apart: 9 -> 8, of which waited for: 3 -> 7; matrix products, arithmetic and copies ran while one was open for 21% -> 16% of each run, Pallas kernels for 0% -> 0%
where the time goes in v3:
time: 481 us; the launch traced here: 476 us
  waiting for transfers between devices  225 us (47%)
  local copies, waits for them, and re-layouts  114 us (24%)
  starting transfers between devices  56.4 us (12%)
  matrix products  24.6 us (5%)
  blocking collectives  20.8 us (4%)
  other arithmetic  19.9 us (4%)
  between operations  14.7 us (3%)
    all_gather x3, waiting for transfers between devices, gather_weights(): block = lax.all_gather(block, axis, axis=dim, tiled=True)  181 us
    unnamed x36, local copies, waits for them, and re-layouts  31 us
    all_to_all x1, waiting for transfers between devices, scatter_grad(): lax.all_to_all(blocks.astype(jnp.bfloat16), DP + SEQ, 0, 0, tiled=True)  23.8 us
    all_gather x2, blocking collectives, gather_weights(): block = lax.all_gather(block, axis, axis=dim, tiled=True)  20.8 us
    slice x2, local copies, waits for them, and re-layouts, gather_weights(): piece = block[:, start:start + rows]  18.9 us
    all_to_all x1, starting transfers between devices, scatter_grad(): lax.all_to_all(blocks.astype(jnp.bfloat16), DP + SEQ, 0, 0, tiled=True)  18.2 us
    reshape x1, local copies, waits for them, and re-layouts, gather_weights(): block = block.reshape(seq, -1, dp * width)  16.2 us
    another operation x2, local copies, waits for them, and re-layouts, gather_weights(): outs.append(piece.reshape(seq * rows, dp * cols))  15.4 us
  transfers between devices with their start and end apart: 8, of which 7 were waited for; matrix products, arithmetic and copies ran while one was open for 16% of the time, Pallas kernels for 0%

profile of v3, /device:TPU:1, one launch (start us, length us, event | category | flops | bytes accessed | tf_op | source)
XLA Modules:
  0.0 475.9 jit_solution(9579186918541707810)
XLA Ops:
  8.0 8.3 %all-gather = bf16[2,216,54]{1,2,0:T(8,128)(2,1)S(1)} all-gather(bf16[1,216,54]{1,2,0:T(8,128)(2,1)S(1)} %fusion.55), channel_id=1, replica_groups=mesh['zh'=4,'core'=2,'x'=4,'zl'=2,'y'=8] {'core'}, dimensions={0}, use_global_device_ids=true | all-gather | bytes 69984 | tf_op jit(solution)/shard_map/all_gather | solution.py:21
  16.5 12.4 %all-gather.1 = bf16[4,432,54]{1,2,0:T(8,128)(2,1)S(1)} all-gather(bf16[1,432,54]{1,2,0:T(8,128)(2,1)S(1)} %reshape.578), channel_id=1, replica_groups=mesh['zh'=4,'core'=2,'x'=4,'zl'=2,'y'=8] {'zh'}, dimensions={0}, use_global_device_ids=true | all-gather | bytes 233280 | tf_op jit(solution)/shard_map/all_gather | solution.py:21
  29.1 1.0 reshape.579
  30.1 39.4 %all-gather.11.cloned.1.call-done = bf16[8,54,1728]{2,1,0:T(8,128)(2,1)} async-done(((bf16[1,54,1728]{2,1,0:T(8,128)(2,1)}), bf16[8,54,1728]{2,1,0:T(8,128)(2,1)}) %all-gather.11.cloned.1.call-update) | async-done | bytes 1493008 | tf_op jit(solution)/shard_map/all_gather | solution.py:21
  69.5 2.7 reshape.581
  72.3 55.5 %all-gather.7.cloned.1.call-done = bf16[864,1728]{1,0:T(8,128)(2,1)} async-done(((bf16[432,1728]{1,0:T(8,128)(2,1)}), bf16[864,1728]{1,0:T(8,128)(2,1)}) %all-gather.7.cloned.1.call-update) | async-done | bytes 2986000 | tf_op jit(solution)/shard_map/all_gather | solution.py:21
  127.8 1.0 copy.83
  128.8 9.9 %all-to-all-start = ((bf16[1,2,64,1152]{3,1,0,2:T(2,128)(2,1)}), bf16[1,2,64,1152]{3,1,0,2:T(2,128)(2,1)S(1)}, u32[]{:S(2)}, u32[]{:S(2)}) async-start(bf16[1,2,64,1152]{3,1,0,2:T(2,128)(2,1)} %copy.83), calls=%async_computation | async-start | bytes 589824 | tf_op jit(solution)/shard_map/all_to_all | solution.py:98
  138.7 1.0 copy.99
  139.7 11.0 %all-to-all-done = bf16[1,2,64,1152]{3,1,0,2:T(2,128)(2,1)S(1)} async-done(((bf16[1,2,64,1152]{3,1,0,2:T(2,128)(2,1)}), bf16[1,2,64,1152]{3,1,0,2:T(2,128)(2,1)S(1)}, u32[]{:S(2)}, u32[]{:S(2)}) %all-to-all-start) | async-done | bytes 294944 | tf_op jit(solution)/shard_map/all_to_all | solution.py:98
  150.7 6.4 %all-to-all-start.2 = ((bf16[1,2,64,1152]{3,1,0,2:T(2,128)(2,1)}), bf16[1,2,64,1152]{3,1,0,2:T(2,128)(2,1)S(1)}, u32[]{:S(2)}, u32[]{:S(2)}) async-start(bf16[1,2,64,1152]{3,1,0,2:T(2,128)(2,1)} %copy.99), calls=%async_computation.2 | async-start | bytes 589824 | tf_op jit(solution)/shard_map/all_to_all | solution.py:112
  159.4 9.0 %all-to-all-done.2 = bf16[1,2,64,1152]{3,1,0,2:T(2,128)(2,1)S(1)} async-done(((bf16[1,2,64,1152]{3,1,0,2:T(2,128)(2,1)}), bf16[1,2,64,1152]{3,1,0,2:T(2,128)(2,1)S(1)}, u32[]{:S(2)}, u32[]{:S(2)}) %all-to-all-start.2) | async-done | bytes 294944 | tf_op jit(solution)/shard_map/all_to_all | solution.py:112
  168.5 0.9 copy.110
  169.9 85.8 %all-gather.9.cloned.1.call-done = bf16[3456,1728]{1,0:T(8,128)(2,1)} async-done(((bf16[864,1728]{1,0:T(8,128)(2,1)}), bf16[3456,1728]{1,0:T(8,128)(2,1)}) %all-gather.9.cloned.1.call-update) | async-done | bytes 11943952 | tf_op jit(solution)/shard_map/all_gather | solution.py:21
  255.6 16.2 %reshape.541 = bf16[64,54,1728]{2,1,0:T(8,128)(2,1)} reshape(bf16[3456,1728]{1,0:T(8,128)(2,1)} %all-gather.9.cloned.1.call-done) | data formatting | bytes 23887872 | tf_op jit(solution)/shard_map/reshape | solution.py:23
  271.8 11.4 %fusion.69 = (bf16[64,18,1728]{2,1,0:T(8,128)(2,1)}, bf16[64,18,1728]{2,1,0:T(8,128)(2,1)}) fusion(bf16[64,54,1728]{2,1,0:T(8,128)(2,1)} %reshape.541), kind=kLoop, calls=%fused_computation.133 | loop fusion | bytes 15925248 | tf_op jit(solution)/shard_map/slice | solution.py:28
  283.2 7.5 %fusion.68 = (bf16[64,9,1728]{2,1,0:T(8,128)(2,1)}, bf16[64,9,1728]{2,1,0:T(8,128)(2,1)}) fusion(bf16[64,54,1728]{2,1,0:T(8,128)(2,1)} %reshape.541), kind=kLoop, calls=%fused_computation.132 | loop fusion | bytes 7962624 | tf_op jit(solution)/shard_map/slice | solution.py:28
  290.7 7.7 %reshape_reshape.9 = bf16[1152,1728]{1,0:T(8,128)(2,1)} reshape(bf16[64,18,1728]{2,1,0:T(8,128)(2,1)} %get-tuple-element.18) | data formatting | bytes 7962624 | tf_op jit(solution)/shard_map/reshape;reshape | solution.py:31
  298.4 3.8 convolution_convert_fusion.5
  302.6 7.2 %reshape.547 = bf16[576,8,216]{2,1,0:T(8,128)(2,1)} reshape(bf16[64,9,1728]{2,1,0:T(8,128)(2,1)} %get-tuple-element.16) | data formatting | bytes 3981312 | tf_op jit(solution)/shard_map/reshape | solution.py:30
  309.8 4.0 copy.89
  317.7 2.4 reduce.29
  320.9 10.7 %all-to-all-start.1 = ((bf16[64,2,1152]{2,1,0:T(2,128)(2,1)}), bf16[64,2,1152]{2,1,0:T(2,128)(2,1)S(1)}, u32[]{:S(2)}, u32[]{:S(2)}) async-start(bf16[64,2,1152]{2,1,0:T(2,128)(2,1)} %reshape.586), calls=%async_computation.1 | async-start | bytes 589824 | tf_op jit(solution)/shard_map/all_to_all | solution.py:102
  331.6 7.7 %reshape_reshape.10 = bf16[1152,1728]{1,0:T(8,128)(2,1)} reshape(bf16[64,18,1728]{2,1,0:T(8,128)(2,1)} %get-tuple-element.17) | data formatting | bytes 7962624 | tf_op jit(solution)/shard_map/reshape;reshape | solution.py:31
  339.3 7.2 %reshape.555 = bf16[576,8,216]{2,1,0:T(8,128)(2,1)} reshape(bf16[64,9,1728]{2,1,0:T(8,128)(2,1)} %get-tuple-element.15) | data formatting | bytes 3981312 | tf_op jit(solution)/shard_map/reshape | solution.py:30
  346.4 3.8 copy.98
  350.3 3.8 multiply_reduce_fusion
  354.7 2.4 reduce.28
  358.8 3.5 copy.112
  362.3 9.3 %reshape.590 = bf16[512,2,648]{2,1,0:T(2,128)(2,1)} reshape(bf16[512,9,144]{2,1,0:T(8,128)(2,1)} %copy.112) | data formatting | bytes 2654208
  371.6 11.1 %all-to-all-start.3 = ((bf16[64,2,1152]{2,1,0:T(2,128)(2,1)}), bf16[64,2,1152]{2,1,0:T(2,128)(2,1)}, u32[]{:S(2)}, u32[]{:S(2)}) async-start(bf16[64,2,1152]{2,1,0:T(2,128)(2,1)} %reshape.588), calls=%async_computation.3 | async-start | bytes 589824 | tf_op jit(solution)/shard_map/all_to_all | solution.py:116
  383.6 1.1 fusion.15
  384.9 3.8 convolution_convert_fusion.3
  389.1 1.3 fusion.70
  390.4 1.2 copy.127
  394.4 18.2 %all-to-all-start.4 = ((bf16[512,2,648]{2,1,0:T(2,128)(2,1)}), bf16[512,2,648]{2,1,0:T(2,128)(2,1)S(1)}, u32[]{:S(2)}, u32[]{:S(2)}) async-start(bf16[512,2,648]{2,1,0:T(2,128)(2,1)} %reshape.590), calls=%async_computation.4 | async-start | bytes 3145728 | tf_op jit(solution)/shard_map/all_to_all | solution.py:40
  412.6 3.0 reshape.589
  415.6 1.7 convert.18
  417.8 1.9 fusion.20
  420.9 1.5 convert_reduce_fusion.1
  422.4 1.2 fusion.65
  423.6 1.2 fusion.8
  424.9 1.2 fusion.7
  427.6 3.6 fusion
  431.4 1.9 add_convert_fusion
  433.3 23.8 %all-to-all-done.4 = bf16[512,2,648]{2,1,0:T(2,128)(2,1)S(1)} async-done(((bf16[512,2,648]{2,1,0:T(2,128)(2,1)}), bf16[512,2,648]{2,1,0:T(2,128)(2,1)S(1)}, u32[]{:S(2)}, u32[]{:S(2)}) %all-to-all-start.4) | async-done | bytes 1327136 | tf_op jit(solution)/shard_map/all_to_all | solution.py:40
  457.1 8.1 %reshape.591 = bf16[512,9,144]{2,1,0:T(8,128)(2,1)} reshape(bf16[512,2,648]{2,1,0:T(2,128)(2,1)S(1)} %all-to-all-done.4) | data formatting | bytes 2654208
  465.2 3.7 convert_reduce_fusion
  (91 shorter events, 18.8 us)
Async XLA Ops:
  7.2 62.3 %all-gather.11.cloned.1.call-start = ((), (), s32[]{:S(2)}) async-start(), calls=%async_computation.7 | async-start | bytes 1806336 | tf_op jit(solution)/shard_map/all_gather | solution.py:21
  29.0 98.7 %copy-start.5 = (bf16[1,2,64,1152]{3,2,1,0:T(8,128)(2,1)S(1)}, bf16[1,2,64,1152]{3,2,1,0:T(8,128)(2,1)}, u32[]{:S(2)}) copy-start(bf16[1,2,64,1152]{3,2,1,0:T(8,128)(2,1)} %param.8) | copy-start | bytes 884740
  30.0 108.6 %copy-start.6 = (bf16[1,2,64,1152]{3,2,1,0:T(8,128)(2,1)S(1)}, bf16[1,2,64,1152]{3,2,1,0:T(8,128)(2,1)}, u32[]{:S(2)}) copy-start(bf16[1,2,64,1152]{3,2,1,0:T(8,128)(2,1)} %param.11) | copy-start | bytes 884740
  30.0 97.7 %all-gather.7.cloned.1.call-start = ((), (), s32[]{:S(2)}) async-start(), calls=%async_computation.5 | async-start | bytes 4644864 | tf_op jit(solution)/shard_map/all_gather | solution.py:21
  72.2 183.4 %all-gather.9.cloned.1.call-start = ((), (), s32[]{:S(2)}) async-start(), calls=%async_computation.6 | async-start | bytes 15482880 | tf_op jit(solution)/shard_map/all_gather | solution.py:21
  128.8 21.9 %all-to-all-start = ((bf16[1,2,64,1152]{3,1,0,2:T(2,128)(2,1)}), bf16[1,2,64,1152]{3,1,0,2:T(2,128)(2,1)S(1)}, u32[]{:S(2)}, u32[]{:S(2)}) async-start(bf16[1,2,64,1152]{3,1,0,2:T(2,128)(2,1)} %copy.83), calls=%async_computation | async-start | bytes 589824 | tf_op jit(solution)/shard_map/all_to_all | solution.py:98
  150.7 17.7 %all-to-all-start.2 = ((bf16[1,2,64,1152]{3,1,0,2:T(2,128)(2,1)}), bf16[1,2,64,1152]{3,1,0,2:T(2,128)(2,1)S(1)}, u32[]{:S(2)}, u32[]{:S(2)}) async-start(bf16[1,2,64,1152]{3,1,0,2:T(2,128)(2,1)} %copy.99), calls=%async_computation.2 | async-start | bytes 589824 | tf_op jit(solution)/shard_map/all_to_all | solution.py:112
  320.9 50.7 %all-to-all-start.1 = ((bf16[64,2,1152]{2,1,0:T(2,128)(2,1)}), bf16[64,2,1152]{2,1,0:T(2,128)(2,1)S(1)}, u32[]{:S(2)}, u32[]{:S(2)}) async-start(bf16[64,2,1152]{2,1,0:T(2,128)(2,1)} %reshape.586), calls=%async_computation.1 | async-start | bytes 589824 | tf_op jit(solution)/shard_map/all_to_all | solution.py:102
  350.3 7.7 %copy-start.7 = (bf16[1152,128]{1,0:T(8,128)(2,1)S(1)}, bf16[1152,128]{1,0:T(8,128)(2,1)}, u32[]{:S(2)}) copy-start(bf16[1152,128]{1,0:T(8,128)(2,1)} %copy.110) | copy-start | bytes 884740
  371.6 22.7 %all-to-all-start.3 = ((bf16[64,2,1152]{2,1,0:T(2,128)(2,1)}), bf16[64,2,1152]{2,1,0:T(2,128)(2,1)}, u32[]{:S(2)}, u32[]{:S(2)}) async-start(bf16[64,2,1152]{2,1,0:T(2,128)(2,1)} %reshape.588), calls=%async_computation.3 | async-start | bytes 589824 | tf_op jit(solution)/shard_map/all_to_all | solution.py:116
  384.8 46.6 %copy-start.2 = (bf16[1,2,64,1152]{3,2,1,0:T(8,128)(2,1)}, bf16[1,2,64,1152]{3,2,1,0:T(8,128)(2,1)S(1)}, u32[]{:S(2)}) copy-start(bf16[1,2,64,1152]{3,2,1,0:T(8,128)(2,1)S(1)} %get-tuple-element.14) | copy-start | bytes 884740
  391.6 2.8 copy-start.3
  391.8 2.5 copy-start.4
  392.0 0.7 copy-start.9
  392.3 0.8 copy-start
  394.4 62.7 %all-to-all-start.4 = ((bf16[512,2,648]{2,1,0:T(2,128)(2,1)}), bf16[512,2,648]{2,1,0:T(2,128)(2,1)S(1)}, u32[]{:S(2)}, u32[]{:S(2)}) async-start(bf16[512,2,648]{2,1,0:T(2,128)(2,1)} %reshape.590), calls=%async_computation.4 | async-start | bytes 3145728 | tf_op jit(solution)/shard_map/all_to_all | solution.py:40
  419.7 0.7 copy-start.8
  420.4 5.6 %copy-start.1 = (f32[2,8,64,64]{2,3,1,0:T(8,128)S(1)}, f32[2,8,64,64]{2,3,1,0:T(8,128)}, u32[]{:S(2)}) copy-start(f32[2,8,64,64]{2,3,1,0:T(8,128)} %copy-done) | copy-start | bytes 786436
Sparse Core Ops, SparseCore 0:
  30.2 39.2 all-gather.10
  72.3 55.3 all-gather.6
  129.8 125.7 all-gather.8

commit v4 on v2

--- a/solution.py
+++ b/solution.py
@@ -23,7 +23,8 @@
     dp, seq = lax.axis_size(DP), lax.axis_size(SEQ)
     blocks = partial.reshape(seq, rows // seq, dp, cols // dp).transpose(2, 0, 1, 3)
     blocks = blocks.reshape(dp * seq, rows // seq, cols // dp)
-    return lax.all_to_all(blocks, DP + SEQ, 0, 0, tiled=True).sum(0)
+    sent = lax.all_to_all(blocks.astype(jnp.bfloat16), DP + SEQ, 0, 0, tiled=True)
+    return sent.astype(jnp.float32).sum(0)
 
 
 def for_sending(shard):
@@ -67,8 +68,8 @@
 def body(
     y_first, y_second, grad_first, grad_second, w_qkv_space, w_out_space, w_qkv_time, w_out_time
 ):
-    space_qkv, space_proj, time_qkv, time_proj = (
-        gather_weight(w) for w in (w_qkv_space, w_out_space, w_qkv_time, w_out_time)
+    time_qkv, time_proj, space_qkv, space_proj = (
+        gather_weight(w) for w in (w_qkv_time, w_out_time, w_qkv_space, w_out_space)
     )
     frame_count = y_first.shape[1]
     tokens = y_first.shape[2]

time: 429 us -> 390 us (0.909)
  local copies, waits for them, and re-layouts: 56.2 us -> 40.9 us
  other arithmetic: 28.1 us -> 12.9 us
  waiting for transfers between devices: 40.8 us -> 35.7 us
    all_to_all x1 -> x0, other arithmetic: 10.1 us -> none  [scatter_grad(): return lax.all_to_all(blocks, DP + SEQ, 0, 0, tiled=True).sum(0)]
    all_to_all x1, waiting for transfers between devices: 27.3 us -> 18.6 us  [scatter_grad(): lax.all_to_all(blocks.astype(jnp.bfloat16), DP + SEQ, 0, 0, tiled=True)]
    unnamed x73 -> x57, local copies, waits for them, and re-layouts: 32.4 us -> 25.7 us
    reshape x1 -> x0, local copies, waits for them, and re-layouts: 6.19 us -> none  [scatter_grad(): blocks = blocks.reshape(dp * seq, rows // seq, cols // dp)]
    all_to_all x1, starting transfers between devices: 4.84 us -> 10.8 us  [body(): lax.all_to_all(for_sending(time_out), SEQ, split_axis=1, concat_axis=2, t...]
  transfers between devices with their start and end apart: 9 -> 9, of which waited for: 3 -> 3; matrix products, arithmetic and copies ran while one was open for 21% -> 17% of each run, Pallas kernels for 0% -> 0%
where the time goes in v4:
time: 390 us; the launch traced here: 384 us
  blocking collectives  198 us (51%)
  starting transfers between devices  56.3 us (14%)
  local copies, waits for them, and re-layouts  40.9 us (10%)
  waiting for transfers between devices  35.7 us (9%)
  matrix products  25 us (6%)
  between operations  14.9 us (4%)
  other arithmetic  12.9 us (3%)
    all_gather x16, blocking collectives, gather_weight(): shard = lax.all_gather(shard, axis, axis=dim, tiled=True)  198 us
    unnamed x57, local copies, waits for them, and re-layouts  25.7 us
    all_to_all x1, starting transfers between devices, scatter_grad(): lax.all_to_all(blocks.astype(jnp.bfloat16), DP + SEQ, 0, 0, tiled=True)  21.3 us
    all_to_all x1, waiting for transfers between devices, scatter_grad(): lax.all_to_all(blocks.astype(jnp.bfloat16), DP + SEQ, 0, 0, tiled=True)  18.6 us
    dot_general x4, matrix products, attend(): jnp.dot(normed, w_qkv, preferred_element_type=jnp.float32)  12.9 us
    all_to_all x1, starting transfers between devices, body(): lax.all_to_all(for_sending(time_out), SEQ, split_axis=1, concat_axis=2, t...  10.8 us
    all_to_all x1, waiting for transfers between devices, body(): lax.all_to_all(grad_second, SEQ, split_axis=2, concat_axis=1, tiled=True)  9.88 us
    all_to_all x1, starting transfers between devices, body(): lax.all_to_all(y_first, SEQ, split_axis=2, concat_axis=1, tiled=True)  9.59 us
  transfers between devices with their start and end apart: 9, of which 3 were waited for; matrix products, arithmetic and copies ran while one was open for 17% of the time, Pallas kernels for 0%

profile of v4, /device:TPU:1, one launch (start us, length us, event | category | flops | bytes accessed | tf_op | source)
XLA Modules:
  0.0 384.2 jit_solution(622644478321903925)
XLA Ops:
  7.2 8.5 %all-gather.3 = bf16[2,144,9]{1,2,0:T(8,128)(2,1)S(1)} all-gather(bf16[1,144,9]{1,2,0:T(8,128)(2,1)} %bitcast.262), channel_id=1, replica_groups=mesh['zh'=4,'core'=2,'x'=4,'zl'=2,'y'=8] {'core'}, dimensions={0}, use_global_device_ids=true | all-gather | bytes 7776 | tf_op jit(solution)/shard_map/all_gather | solution.py:17
  15.9 11.2 %all-gather.4 = bf16[4,288,9]{1,2,0:T(8,128)(2,1)S(1)} all-gather(bf16[1,288,9]{1,2,0:T(8,128)(2,1)S(1)} %reshape.521), channel_id=1, replica_groups=mesh['zh'=4,'core'=2,'x'=4,'zl'=2,'y'=8] {'zh'}, dimensions={0}, use_global_device_ids=true | all-gather | bytes 25920 | tf_op jit(solution)/shard_map/all_gather | solution.py:17
  27.1 20.5 %all-gather.5 = bf16[8,9,1152]{2,1,0:T(8,128)(2,1)S(1)} all-gather(bf16[1,9,1152]{2,1,0:T(8,128)(2,1)S(1)} %bitcast.258), channel_id=1, replica_groups=mesh['zh'=4,'core'=2,'x'=4,'zl'=2,'y'=8] {'y'}, dimensions={0}, use_global_device_ids=true | all-gather | bytes 186624 | tf_op jit(solution)/shard_map/all_gather | solution.py:17
  47.7 5.2 %all_gather.68 = bf16[144,1152]{1,0:T(8,128)(2,1)} all-gather(bf16[72,1152]{1,0:T(8,128)(2,1)S(1)} %reshape.524), channel_id=1, replica_groups=mesh['zh'=4,'core'=2,'x'=4,'zl'=2,'y'=8] {'zl'}, dimensions={0}, use_global_device_ids=true | all-gather | bytes 497664 | tf_op jit(solution)/shard_map/all_gather | solution.py:17
  52.9 11.6 %all-gather = bf16[2,216,18]{1,2,0:T(8,128)(2,1)S(1)} all-gather(bf16[1,216,18]{1,2,0:T(8,128)(2,1)} %bitcast.260), channel_id=1, replica_groups=mesh['zh'=4,'core'=2,'x'=4,'zl'=2,'y'=8] {'core'}, dimensions={0}, use_global_device_ids=true | all-gather | bytes 23328 | tf_op jit(solution)/shard_map/all_gather | solution.py:17
  64.6 11.2 %all-gather.1 = bf16[4,432,18]{1,2,0:T(8,128)(2,1)S(1)} all-gather(bf16[1,432,18]{1,2,0:T(8,128)(2,1)S(1)} %reshape.515), channel_id=1, replica_groups=mesh['zh'=4,'core'=2,'x'=4,'zl'=2,'y'=8] {'zh'}, dimensions={0}, use_global_device_ids=true | all-gather | bytes 77760 | tf_op jit(solution)/shard_map/all_gather | solution.py:17
  76.0 21.6 %all-gather.2 = bf16[8,18,1728]{2,1,0:T(8,128)(2,1)S(1)} all-gather(bf16[1,18,1728]{2,1,0:T(8,128)(2,1)S(1)} %bitcast.254), channel_id=1, replica_groups=mesh['zh'=4,'core'=2,'x'=4,'zl'=2,'y'=8] {'y'}, dimensions={0}, use_global_device_ids=true | all-gather | bytes 559872 | tf_op jit(solution)/shard_map/all_gather | solution.py:17
  97.9 8.7 %all_gather.63 = bf16[288,1728]{1,0:T(8,128)(2,1)} all-gather(bf16[144,1728]{1,0:T(8,128)(2,1)S(1)} %reshape.518), channel_id=1, replica_groups=mesh['zh'=4,'core'=2,'x'=4,'zl'=2,'y'=8] {'zl'}, dimensions={0}, use_global_device_ids=true | all-gather | bytes 1492992 | tf_op jit(solution)/shard_map/all_gather | solution.py:17
  106.7 10.0 %all-gather.9 = bf16[2,144,9]{1,2,0:T(8,128)(2,1)S(1)} all-gather(bf16[1,144,9]{1,2,0:T(8,128)(2,1)S(1)} %bitcast.263), channel_id=1, replica_groups=mesh['zh'=4,'core'=2,'x'=4,'zl'=2,'y'=8] {'core'}, dimensions={0}, use_global_device_ids=true | all-gather | bytes 7776 | tf_op jit(solution)/shard_map/all_gather | solution.py:17
  116.8 11.1 %all-gather.10 = bf16[4,288,9]{1,2,0:T(8,128)(2,1)S(1)} all-gather(bf16[1,288,9]{1,2,0:T(8,128)(2,1)S(1)} %reshape.533), channel_id=1, replica_groups=mesh['zh'=4,'core'=2,'x'=4,'zl'=2,'y'=8] {'zh'}, dimensions={0}, use_global_device_ids=true | all-gather | bytes 25920 | tf_op jit(solution)/shard_map/all_gather | solution.py:17
  128.0 21.3 %all-gather.11 = bf16[8,9,1152]{2,1,0:T(8,128)(2,1)S(1)} all-gather(bf16[1,9,1152]{2,1,0:T(8,128)(2,1)S(1)} %bitcast.259), channel_id=1, replica_groups=mesh['zh'=4,'core'=2,'x'=4,'zl'=2,'y'=8] {'y'}, dimensions={0}, use_global_device_ids=true | all-gather | bytes 186624 | tf_op jit(solution)/shard_map/all_gather | solution.py:17
  149.4 5.3 %all_gather.78 = bf16[144,1152]{1,0:T(8,128)(2,1)} all-gather(bf16[72,1152]{1,0:T(8,128)(2,1)S(1)} %reshape.536), channel_id=1, replica_groups=mesh['zh'=4,'core'=2,'x'=4,'zl'=2,'y'=8] {'zl'}, dimensions={0}, use_global_device_ids=true | all-gather | bytes 497664 | tf_op jit(solution)/shard_map/all_gather | solution.py:17
  154.7 1.0 copy.189
  155.7 9.6 %all-to-all-start = ((bf16[1,2,64,1152]{3,1,0,2:T(2,128)(2,1)}), bf16[1,2,64,1152]{3,1,0,2:T(2,128)(2,1)S(1)}, u32[]{:S(2)}, u32[]{:S(2)}) async-start(bf16[1,2,64,1152]{3,1,0,2:T(2,128)(2,1)} %copy.189), calls=%async_computation | async-start | bytes 589824 | tf_op jit(solution)/shard_map/all_to_all | solution.py:84
  165.4 9.4 %all-gather.6 = bf16[2,216,18]{1,2,0:T(8,128)(2,1)S(1)} all-gather(bf16[1,216,18]{1,2,0:T(8,128)(2,1)S(1)} %bitcast.261), channel_id=1, replica_groups=mesh['zh'=4,'core'=2,'x'=4,'zl'=2,'y'=8] {'core'}, dimensions={0}, use_global_device_ids=true | all-gather | bytes 23328 | tf_op jit(solution)/shard_map/all_gather | solution.py:17
  174.9 11.7 %all-gather.7 = bf16[4,432,18]{1,2,0:T(8,128)(2,1)S(1)} all-gather(bf16[1,432,18]{1,2,0:T(8,128)(2,1)S(1)} %reshape.527), channel_id=1, replica_groups=mesh['zh'=4,'core'=2,'x'=4,'zl'=2,'y'=8] {'zh'}, dimensions={0}, use_global_device_ids=true | all-gather | bytes 77760 | tf_op jit(solution)/shard_map/all_gather | solution.py:17
  186.7 22.6 %all-gather.8 = bf16[8,18,1728]{2,1,0:T(8,128)(2,1)S(1)} all-gather(bf16[1,18,1728]{2,1,0:T(8,128)(2,1)S(1)} %bitcast.255), channel_id=1, replica_groups=mesh['zh'=4,'core'=2,'x'=4,'zl'=2,'y'=8] {'y'}, dimensions={0}, use_global_device_ids=true | all-gather | bytes 559872 | tf_op jit(solution)/shard_map/all_gather | solution.py:17
  209.6 8.7 %all_gather.73 = bf16[288,1728]{1,0:T(8,128)(2,1)} all-gather(bf16[144,1728]{1,0:T(8,128)(2,1)S(1)} %reshape.530), channel_id=1, replica_groups=mesh['zh'=4,'core'=2,'x'=4,'zl'=2,'y'=8] {'zl'}, dimensions={0}, use_global_device_ids=true | all-gather | bytes 1492992 | tf_op jit(solution)/shard_map/all_gather | solution.py:17
  218.4 1.0 copy.209
  219.4 9.5 %all-to-all-start.2 = ((bf16[1,2,64,1152]{3,1,0,2:T(2,128)(2,1)}), bf16[1,2,64,1152]{3,1,0,2:T(2,128)(2,1)S(1)}, u32[]{:S(2)}, u32[]{:S(2)}) async-start(bf16[1,2,64,1152]{3,1,0,2:T(2,128)(2,1)} %copy.209), calls=%async_computation.2 | async-start | bytes 589824 | tf_op jit(solution)/shard_map/all_to_all | solution.py:98
  230.3 9.9 %all-to-all-done.2 = bf16[1,2,64,1152]{3,1,0,2:T(2,128)(2,1)S(1)} async-done(((bf16[1,2,64,1152]{3,1,0,2:T(2,128)(2,1)}), bf16[1,2,64,1152]{3,1,0,2:T(2,128)(2,1)S(1)}, u32[]{:S(2)}, u32[]{:S(2)}) %all-to-all-start.2) | async-done | bytes 294944 | tf_op jit(solution)/shard_map/all_to_all | solution.py:98
  240.5 2.0 convolution_convert_fusion.18
  242.5 3.8 convolution_convert_fusion.5
  248.5 1.5 multiply_reduce_fusion
  251.2 2.4 reduce.29
  254.4 4.9 %all-to-all-start.3 = ((bf16[64,2,1152]{2,1,0:T(2,128)(2,1)}), bf16[64,2,1152]{2,1,0:T(2,128)(2,1)S(1)}, u32[]{:S(2)}, u32[]{:S(2)}) async-start(bf16[64,2,1152]{2,1,0:T(2,128)(2,1)} %reshape.546), calls=%async_computation.3 | async-start | bytes 589824 | tf_op jit(solution)/shard_map/all_to_all | solution.py:102
  260.5 2.4 reduce.28
  264.6 3.5 copy.222
  268.1 9.3 %reshape.548 = bf16[512,2,648]{2,1,0:T(2,128)(2,1)} reshape(bf16[512,9,144]{2,1,0:T(8,128)(2,1)} %copy.222) | data formatting | bytes 2654208
  277.5 10.8 %all-to-all-start.1 = ((bf16[64,2,1152]{2,1,0:T(2,128)(2,1)}), bf16[64,2,1152]{2,1,0:T(2,128)(2,1)S(1)}, u32[]{:S(2)}, u32[]{:S(2)}) async-start(bf16[64,2,1152]{2,1,0:T(2,128)(2,1)} %reshape.544), calls=%async_computation.1 | async-start | bytes 589824 | tf_op jit(solution)/shard_map/all_to_all | solution.py:88
  289.3 2.0 convolution_convert_fusion.17
  291.4 1.0 reshape.499
  292.4 7.1 %all-to-all-done.1 = bf16[64,2,1152]{2,1,0:T(2,128)(2,1)S(1)} async-done(((bf16[64,2,1152]{2,1,0:T(2,128)(2,1)}), bf16[64,2,1152]{2,1,0:T(2,128)(2,1)S(1)}, u32[]{:S(2)}, u32[]{:S(2)}) %all-to-all-start.1) | async-done | bytes 294944 | tf_op jit(solution)/shard_map/all_to_all | solution.py:88
  299.5 21.3 %all-to-all-start.4 = ((bf16[512,2,648]{2,1,0:T(2,128)(2,1)}), bf16[512,2,648]{2,1,0:T(2,128)(2,1)S(1)}, u32[]{:S(2)}, u32[]{:S(2)}) async-start(bf16[512,2,648]{2,1,0:T(2,128)(2,1)} %reshape.548), calls=%async_computation.4 | async-start | bytes 3145728 | tf_op jit(solution)/shard_map/all_to_all | solution.py:26
  322.2 3.8 convolution_convert_fusion.3
  326.4 1.3 fusion.58
  328.5 1.2 copy.234
  329.7 1.4 convert_reduce_fusion.1
  331.9 1.2 fusion.6
  333.3 1.4 copy.219
  334.7 2.5 reshape.501
  337.2 1.3 fusion.5
  339.4 1.9 reshape.494
  341.3 3.8 fusion
  345.7 1.1 fusion.16
  346.8 18.6 %all-to-all-done.4 = bf16[512,2,648]{2,1,0:T(2,128)(2,1)S(1)} async-done(((bf16[512,2,648]{2,1,0:T(2,128)(2,1)}), bf16[512,2,648]{2,1,0:T(2,128)(2,1)S(1)}, u32[]{:S(2)}, u32[]{:S(2)}) %all-to-all-start.4) | async-done | bytes 1327136 | tf_op jit(solution)/shard_map/all_to_all | solution.py:26
  365.4 8.1 %reshape.549 = bf16[512,9,144]{2,1,0:T(8,128)(2,1)} reshape(bf16[512,2,648]{2,1,0:T(2,128)(2,1)S(1)} %all-to-all-done.4) | data formatting | bytes 2654208
  373.5 3.7 convert_reduce_fusion
  (124 shorter events, 16.5 us)
Async XLA Ops:
  7.2 99.5 %copy-start.15 = (bf16[9,144]{1,0:T(8,128)(2,1)S(1)}, bf16[9,144]{1,0:T(8,128)(2,1)}, u32[]{:S(2)}) copy-start(bf16[9,144]{1,0:T(8,128)(2,1)} %param.13) | copy-start | bytes 7780
  7.2 233.3 %all-gather.19.cloned.1.call-start = ((), (), s32[]{:S(2)}) async-start(), calls=%async_computation.6 | async-start | bytes 1658880 | tf_op jit(solution)/shard_map/all_gather | solution.py:17
  47.6 107.1 %copy-start.6 = (bf16[1,2,64,1152]{3,2,1,0:T(8,128)(2,1)S(1)}, bf16[1,2,64,1152]{3,2,1,0:T(8,128)(2,1)}, u32[]{:S(2)}) copy-start(bf16[1,2,64,1152]{3,2,1,0:T(8,128)(2,1)} %param.8) | copy-start | bytes 884740
  52.9 112.5 %copy-start.14 = (bf16[18,216]{1,0:T(8,128)(2,1)S(1)}, bf16[18,216]{1,0:T(8,128)(2,1)}, u32[]{:S(2)}) copy-start(bf16[18,216]{1,0:T(8,128)(2,1)} %param.12) | copy-start | bytes 23332
  52.9 189.6 %all-gather.17.cloned.1.call-start = ((), (), s32[]{:S(2)}) async-start(), calls=%async_computation.5 | async-start | bytes 5160960 | tf_op jit(solution)/shard_map/all_gather | solution.py:17
  106.6 111.7 %copy-start.8 = (bf16[1,2,64,1152]{3,2,1,0:T(8,128)(2,1)S(1)}, bf16[1,2,64,1152]{3,2,1,0:T(8,128)(2,1)}, u32[]{:S(2)}) copy-start(bf16[1,2,64,1152]{3,2,1,0:T(8,128)(2,1)} %param.11) | copy-start | bytes 884740
  106.7 182.6 %all-gather.23.cloned.1.call-start = ((), (), s32[]{:S(2)}) async-start(), calls=%async_computation.8 | async-start | bytes 1658880 | tf_op jit(solution)/shard_map/all_gather | solution.py:17
  155.7 63.7 %all-to-all-start = ((bf16[1,2,64,1152]{3,1,0,2:T(2,128)(2,1)}), bf16[1,2,64,1152]{3,1,0,2:T(2,128)(2,1)S(1)}, u32[]{:S(2)}, u32[]{:S(2)}) async-start(bf16[1,2,64,1152]{3,1,0,2:T(2,128)(2,1)} %copy.189), calls=%async_computation | async-start | bytes 589824 | tf_op jit(solution)/shard_map/all_to_all | solution.py:84
  165.3 156.9 %all-gather.21.cloned.1.call-start = ((), (), s32[]{:S(2)}) async-start(), calls=%async_computation.7 | async-start | bytes 5160960 | tf_op jit(solution)/shard_map/all_gather | solution.py:17
  219.4 20.8 %all-to-all-start.2 = ((bf16[1,2,64,1152]{3,1,0,2:T(2,128)(2,1)}), bf16[1,2,64,1152]{3,1,0,2:T(2,128)(2,1)S(1)}, u32[]{:S(2)}, u32[]{:S(2)}) async-start(bf16[1,2,64,1152]{3,1,0,2:T(2,128)(2,1)} %copy.209), calls=%async_computation.2 | async-start | bytes 589824 | tf_op jit(solution)/shard_map/all_to_all | solution.py:98
  246.3 2.2 copy-start
  248.5 11.1 %copy-start.2 = (bf16[576,1152]{1,0:T(8,128)(2,1)S(1)}, bf16[576,1152]{1,0:T(8,128)(2,1)}, u32[]{:S(2)}) copy-start(bf16[576,1152]{1,0:T(8,128)(2,1)} %all-gather.19.cloned.1.call-done) | copy-start | bytes 3981316
  254.4 23.0 %all-to-all-start.3 = ((bf16[64,2,1152]{2,1,0:T(2,128)(2,1)}), bf16[64,2,1152]{2,1,0:T(2,128)(2,1)S(1)}, u32[]{:S(2)}, u32[]{:S(2)}) async-start(bf16[64,2,1152]{2,1,0:T(2,128)(2,1)} %reshape.546), calls=%async_computation.3 | async-start | bytes 589824 | tf_op jit(solution)/shard_map/all_to_all | solution.py:102
  268.1 21.0 %copy-start.11 = (bf16[1,2,64,1152]{3,2,1,0:T(8,128)(2,1)S(1)}, bf16[1,2,64,1152]{3,2,1,0:T(8,128)(2,1)}, u32[]{:S(2)}) copy-start(bf16[1,2,64,1152]{3,2,1,0:T(8,128)(2,1)} %param.10) | copy-start | bytes 884740
  277.5 22.0 %all-to-all-start.1 = ((bf16[64,2,1152]{2,1,0:T(2,128)(2,1)}), bf16[64,2,1152]{2,1,0:T(2,128)(2,1)S(1)}, u32[]{:S(2)}, u32[]{:S(2)}) async-start(bf16[64,2,1152]{2,1,0:T(2,128)(2,1)} %reshape.544), calls=%async_computation.1 | async-start | bytes 589824 | tf_op jit(solution)/shard_map/all_to_all | solution.py:88
  289.2 10.3 %copy-start.5 = (bf16[1,2,64,1152]{3,2,1,0:T(8,128)(2,1)}, bf16[1,2,64,1152]{3,2,1,0:T(8,128)(2,1)S(1)}, u32[]{:S(2)}) copy-start(bf16[1,2,64,1152]{3,2,1,0:T(8,128)(2,1)S(1)} %fusion.15) | copy-start | bytes 884740
  289.3 32.5 %copy-start.12 = (bf16[1,2,64,1152]{3,2,1,0:T(8,128)(2,1)S(1)}, bf16[1,2,64,1152]{3,2,1,0:T(8,128)(2,1)}, u32[]{:S(2)}) copy-start(bf16[1,2,64,1152]{3,2,1,0:T(8,128)(2,1)} %param.9) | copy-start | bytes 884740
  299.5 65.9 %all-to-all-start.4 = ((bf16[512,2,648]{2,1,0:T(2,128)(2,1)}), bf16[512,2,648]{2,1,0:T(2,128)(2,1)S(1)}, u32[]{:S(2)}, u32[]{:S(2)}) async-start(bf16[512,2,648]{2,1,0:T(2,128)(2,1)} %reshape.548), calls=%async_computation.4 | async-start | bytes 3145728 | tf_op jit(solution)/shard_map/all_to_all | solution.py:26
  321.9 5.8 %copy-start.3 = (bf16[1,2,64,1152]{3,2,1,0:T(8,128)(2,1)}, bf16[1,2,64,1152]{3,2,1,0:T(8,128)(2,1)S(1)}, u32[]{:S(2)}) copy-start(bf16[1,2,64,1152]{3,2,1,0:T(8,128)(2,1)S(1)} %get-tuple-element.14) | copy-start | bytes 884740
  329.7 1.6 copy-start.13
  337.2 8.1 %copy-start.1 = (bf16[576,1152]{1,0:T(8,128)(2,1)S(1)}, bf16[576,1152]{1,0:T(8,128)(2,1)}, u32[]{:S(2)}) copy-start(bf16[576,1152]{1,0:T(8,128)(2,1)} %all-gather.23.cloned.1.call-done) | copy-start | bytes 3981316
  338.5 6.6 %copy-start.4 = (bf16[1,2,64,1152]{3,2,1,0:T(8,128)(2,1)S(1)}, bf16[1,2,64,1152]{3,2,1,0:T(8,128)(2,1)}, u32[]{:S(2)}) copy-start(bf16[1,2,64,1152]{3,2,1,0:T(8,128)(2,1)} %copy-done.3) | copy-start | bytes 884740
  339.4 6.3 %copy-start.7 = (bf16[1,2,64,1152]{3,2,1,0:T(8,128)(2,1)S(1)}, bf16[1,2,64,1152]{3,2,1,0:T(8,128)(2,1)}, u32[]{:S(2)}) copy-start(bf16[1,2,64,1152]{3,2,1,0:T(8,128)(2,1)} %param.8) | copy-start | bytes 884740
  341.3 4.0 %copy-start.10 = (bf16[128,576]{1,0:T(8,128)(2,1)S(1)}, bf16[128,576]{1,0:T(8,128)(2,1)}, u32[]{:S(2)}) copy-start(bf16[128,576]{1,0:T(8,128)(2,1)} %reshape.494) | copy-start | bytes 442372
  341.3 4.4 %copy-start.9 = (bf16[1,2,64,1152]{3,2,1,0:T(8,128)(2,1)S(1)}, bf16[1,2,64,1152]{3,2,1,0:T(8,128)(2,1)}, u32[]{:S(2)}) copy-start(bf16[1,2,64,1152]{3,2,1,0:T(8,128)(2,1)} %param.11) | copy-start | bytes 884740
Sparse Core Ops, SparseCore 0:
  53.0 36.2 all-gather.18
  106.8 58.3 all-gather.16
  167.3 30.1 all-gather.22
  218.5 62.7 all-gather.20

commit v5 on v4

--- a/solution.py
+++ b/solution.py
@@ -13,7 +13,7 @@
 
 
 def gather_weight(shard):
-    for axis, dim in (("core", 1), ("zh", 1), ("y", 0), ("zl", 0), ("x", 0)):
+    for axis, dim in ((DP, 1), ("y", 0), (("x", "zl"), 0)):
         shard = lax.all_gather(shard, axis, axis=dim, tiled=True)
     return shard
 

time: 390 us -> 431 us (1.11)
  waiting for transfers between devices: 35.7 us -> 110 us
  blocking collectives: 198 us -> 166 us
    all_gather x4, waiting for transfers between devices: 0.08 us -> 92.5 us  [gather_weight(): shard = lax.all_gather(shard, axis, axis=dim, tiled=True)]
    all_gather x16 -> x8, blocking collectives: 198 us -> 166 us  [gather_weight(): shard = lax.all_gather(shard, axis, axis=dim, tiled=True)]
    all_to_all x1, waiting for transfers between devices: 18.6 us -> 0.01 us  [scatter_grad(): lax.all_to_all(blocks.astype(jnp.bfloat16), DP + SEQ, 0, 0, tiled=True)]
    all_to_all x1, starting transfers between devices: 21.3 us -> 17 us  [scatter_grad(): lax.all_to_all(blocks.astype(jnp.bfloat16), DP + SEQ, 0, 0, tiled=True)]
    unnamed x57 -> x53, local copies, waits for them, and re-layouts: 25.7 us -> 28.2 us
  transfers between devices with their start and end apart: 9 -> 9, of which waited for: 3 -> 3; matrix products, arithmetic and copies ran while one was open for 17% -> 16% of each run, Pallas kernels for 0% -> 0%
where the time goes in v5:
time: 431 us; the launch traced here: 425 us
  blocking collectives  166 us (39%)
  waiting for transfers between devices  110 us (26%)
  starting transfers between devices  53.1 us (12%)
  local copies, waits for them, and re-layouts  43.5 us (10%)
  matrix products  24.8 us (6%)
  between operations  14.6 us (3%)
  other arithmetic  12.9 us (3%)
    all_gather x8, blocking collectives, gather_weight(): shard = lax.all_gather(shard, axis, axis=dim, tiled=True)  166 us
    all_gather x4, waiting for transfers between devices, gather_weight(): shard = lax.all_gather(shard, axis, axis=dim, tiled=True)  92.5 us
    unnamed x53, local copies, waits for them, and re-layouts  28.2 us
    all_to_all x1, starting transfers between devices, scatter_grad(): lax.all_to_all(blocks.astype(jnp.bfloat16), DP + SEQ, 0, 0, tiled=True)  17 us
    dot_general x4, matrix products, attend(): jnp.dot(normed, w_qkv, preferred_element_type=jnp.float32)  12.9 us
    all_to_all x1, starting transfers between devices, body(): lax.all_to_all(for_sending(time_out), SEQ, split_axis=1, concat_axis=2, t...  10.8 us
    all_to_all x1, starting transfers between devices, body(): lax.all_to_all(grad_second, SEQ, split_axis=2, concat_axis=1, tiled=True)  10.3 us
    all_to_all x1, starting transfers between devices, body(): lax.all_to_all(y_first, SEQ, split_axis=2, concat_axis=1, tiled=True)  10 us
  transfers between devices with their start and end apart: 9, of which 3 were waited for; matrix products, arithmetic and copies ran while one was open for 16% of the time, Pallas kernels for 0%

profile of v5, /device:TPU:1, one launch (start us, length us, event | category | flops | bytes accessed | tf_op | source)
XLA Modules:
  0.0 424.6 jit_solution(7813761238031523680)
XLA Ops:
  7.2 21.7 %all-gather.2 = bf16[8,144,9]{1,2,0:T(8,128)(2,1)S(1)} all-gather(bf16[1,144,9]{1,2,0:T(8,128)(2,1)} %bitcast.254), channel_id=1, replica_groups=mesh['zh'=4,'core'=2,'x'=4,'zl'=2,'y'=8] {'zh','core'}, dimensions={0}, use_global_device_ids=true | all-gather | bytes 23328 | tf_op jit(solution)/shard_map/all_gather | solution.py:17
  29.0 20.1 %all-gather.3 = bf16[8,9,1152]{2,1,0:T(8,128)(2,1)S(1)} all-gather(bf16[1,9,1152]{2,1,0:T(8,128)(2,1)S(1)} %bitcast.250), channel_id=1, replica_groups=mesh['zh'=4,'core'=2,'x'=4,'zl'=2,'y'=8] {'y'}, dimensions={0}, use_global_device_ids=true | all-gather | bytes 186624 | tf_op jit(solution)/shard_map/all_gather | solution.py:17
  49.1 0.7 reshape.520
  49.9 21.3 %all-gather = bf16[8,216,18]{1,2,0:T(8,128)(2,1)S(1)} all-gather(bf16[1,216,18]{1,2,0:T(8,128)(2,1)} %bitcast.252), channel_id=1, replica_groups=mesh['zh'=4,'core'=2,'x'=4,'zl'=2,'y'=8] {'zh','core'}, dimensions={0}, use_global_device_ids=true | all-gather | bytes 69984 | tf_op jit(solution)/shard_map/all_gather | solution.py:17
  71.4 22.3 %all-gather.1 = bf16[8,18,1728]{2,1,0:T(8,128)(2,1)S(1)} all-gather(bf16[1,18,1728]{2,1,0:T(8,128)(2,1)S(1)} %bitcast.246), channel_id=1, replica_groups=mesh['zh'=4,'core'=2,'x'=4,'zl'=2,'y'=8] {'y'}, dimensions={0}, use_global_device_ids=true | all-gather | bytes 559872 | tf_op jit(solution)/shard_map/all_gather | solution.py:17
  93.8 1.0 reshape.516
  94.9 18.1 %all-gather.6 = bf16[8,144,9]{1,2,0:T(8,128)(2,1)S(1)} all-gather(bf16[1,144,9]{1,2,0:T(8,128)(2,1)S(1)} %bitcast.255), channel_id=1, replica_groups=mesh['zh'=4,'core'=2,'x'=4,'zl'=2,'y'=8] {'zh','core'}, dimensions={0}, use_global_device_ids=true | all-gather | bytes 23328 | tf_op jit(solution)/shard_map/all_gather | solution.py:17
  113.1 20.1 %all-gather.7 = bf16[8,9,1152]{2,1,0:T(8,128)(2,1)S(1)} all-gather(bf16[1,9,1152]{2,1,0:T(8,128)(2,1)S(1)} %bitcast.251), channel_id=1, replica_groups=mesh['zh'=4,'core'=2,'x'=4,'zl'=2,'y'=8] {'y'}, dimensions={0}, use_global_device_ids=true | all-gather | bytes 186624 | tf_op jit(solution)/shard_map/all_gather | solution.py:17
  133.2 0.7 reshape.528
  134.0 1.0 copy.147
  135.0 10.0 %all-to-all-start = ((bf16[1,2,64,1152]{3,1,0,2:T(2,128)(2,1)}), bf16[1,2,64,1152]{3,1,0,2:T(2,128)(2,1)S(1)}, u32[]{:S(2)}, u32[]{:S(2)}) async-start(bf16[1,2,64,1152]{3,1,0,2:T(2,128)(2,1)} %copy.147), calls=%async_computation | async-start | bytes 589824 | tf_op jit(solution)/shard_map/all_to_all | solution.py:84
  145.1 19.9 %all-gather.4 = bf16[8,216,18]{1,2,0:T(8,128)(2,1)S(1)} all-gather(bf16[1,216,18]{1,2,0:T(8,128)(2,1)S(1)} %bitcast.253), channel_id=1, replica_groups=mesh['zh'=4,'core'=2,'x'=4,'zl'=2,'y'=8] {'zh','core'}, dimensions={0}, use_global_device_ids=true | all-gather | bytes 69984 | tf_op jit(solution)/shard_map/all_gather | solution.py:17
  165.2 22.5 %all-gather.5 = bf16[8,18,1728]{2,1,0:T(8,128)(2,1)S(1)} all-gather(bf16[1,18,1728]{2,1,0:T(8,128)(2,1)S(1)} %bitcast.247), channel_id=1, replica_groups=mesh['zh'=4,'core'=2,'x'=4,'zl'=2,'y'=8] {'y'}, dimensions={0}, use_global_device_ids=true | all-gather | bytes 559872 | tf_op jit(solution)/shard_map/all_gather | solution.py:17
  187.8 1.0 reshape.524
  188.8 1.0 copy.163
  189.9 10.3 %all-to-all-start.2 = ((bf16[1,2,64,1152]{3,1,0,2:T(2,128)(2,1)}), bf16[1,2,64,1152]{3,1,0,2:T(2,128)(2,1)S(1)}, u32[]{:S(2)}, u32[]{:S(2)}) async-start(bf16[1,2,64,1152]{3,1,0,2:T(2,128)(2,1)} %copy.163), calls=%async_computation.2 | async-start | bytes 589824 | tf_op jit(solution)/shard_map/all_to_all | solution.py:98
  201.5 9.9 %all-to-all-done.2 = bf16[1,2,64,1152]{3,1,0,2:T(2,128)(2,1)S(1)} async-done(((bf16[1,2,64,1152]{3,1,0,2:T(2,128)(2,1)}), bf16[1,2,64,1152]{3,1,0,2:T(2,128)(2,1)S(1)}, u32[]{:S(2)}, u32[]{:S(2)}) %all-to-all-start.2) | async-done | bytes 294944 | tf_op jit(solution)/shard_map/all_to_all | solution.py:98
  211.8 1.8 convolution_convert_fusion.18
  213.6 3.8 convolution_convert_fusion.5
  219.6 1.5 multiply_reduce_fusion
  222.3 2.4 reduce.29
  224.7 0.8 reshape.534
  225.6 4.8 %all-to-all-start.3 = ((bf16[64,2,1152]{2,1,0:T(2,128)(2,1)}), bf16[64,2,1152]{2,1,0:T(2,128)(2,1)S(1)}, u32[]{:S(2)}, u32[]{:S(2)}) async-start(bf16[64,2,1152]{2,1,0:T(2,128)(2,1)} %reshape.534), calls=%async_computation.3 | async-start | bytes 589824 | tf_op jit(solution)/shard_map/all_to_all | solution.py:102
  231.5 2.4 reduce.28
  233.9 0.8 reshape.532
  234.8 0.8 convolution_convert_fusion.6
  235.6 3.6 copy.176
  239.2 9.3 %reshape.536 = bf16[512,2,648]{2,1,0:T(2,128)(2,1)} reshape(bf16[512,9,144]{2,1,0:T(8,128)(2,1)} %copy.176) | data formatting | bytes 2654208
  248.6 10.8 %all-to-all-start.1 = ((bf16[64,2,1152]{2,1,0:T(2,128)(2,1)}), bf16[64,2,1152]{2,1,0:T(2,128)(2,1)S(1)}, u32[]{:S(2)}, u32[]{:S(2)}) async-start(bf16[64,2,1152]{2,1,0:T(2,128)(2,1)} %reshape.532), calls=%async_computation.1 | async-start | bytes 589824 | tf_op jit(solution)/shard_map/all_to_all | solution.py:88
  260.4 2.0 convolution_convert_fusion.17
  262.5 1.0 reshape.499
  263.5 7.2 %all-to-all-done.1 = bf16[64,2,1152]{2,1,0:T(2,128)(2,1)S(1)} async-done(((bf16[64,2,1152]{2,1,0:T(2,128)(2,1)}), bf16[64,2,1152]{2,1,0:T(2,128)(2,1)S(1)}, u32[]{:S(2)}, u32[]{:S(2)}) %all-to-all-start.1) | async-done | bytes 294944 | tf_op jit(solution)/shard_map/all_to_all | solution.py:88
  270.7 17.0 %all-to-all-start.4 = ((bf16[512,2,648]{2,1,0:T(2,128)(2,1)}), bf16[512,2,648]{2,1,0:T(2,128)(2,1)S(1)}, u32[]{:S(2)}, u32[]{:S(2)}) async-start(bf16[512,2,648]{2,1,0:T(2,128)(2,1)} %reshape.536), calls=%async_computation.4 | async-start | bytes 3145728 | tf_op jit(solution)/shard_map/all_to_all | solution.py:26
  289.0 92.4 %all-gather.17.cloned.1.call-done = bf16[1152,1728]{1,0:T(8,128)(2,1)} async-done(((bf16[144,1728]{1,0:T(8,128)(2,1)}), bf16[1152,1728]{1,0:T(8,128)(2,1)}) %all-gather.17.cloned.1.call-update) | async-done | bytes 3981328 | tf_op jit(solution)/shard_map/all_gather | solution.py:17
  381.4 3.8 convolution_convert_fusion.3
  385.6 1.3 fusion.58
  387.7 1.2 copy.188
  388.9 1.4 convert_reduce_fusion.1
  391.1 1.2 fusion.6
  392.5 1.4 copy.173
  393.9 2.5 reshape.501
  396.4 1.3 fusion.5
  397.7 0.9 copy.161
  398.6 1.9 reshape.494
  400.5 3.8 fusion
  404.9 1.1 fusion.16
  406.0 8.1 %reshape.537 = bf16[512,9,144]{2,1,0:T(8,128)(2,1)} reshape(bf16[512,2,648]{2,1,0:T(2,128)(2,1)S(1)} %all-to-all-done.4) | data formatting | bytes 2654208
  414.1 3.7 convert_reduce_fusion
  (108 shorter events, 12.1 us)
Async XLA Ops:
  7.2 87.7 %copy-start.15 = (bf16[9,144]{1,0:T(8,128)(2,1)S(1)}, bf16[9,144]{1,0:T(8,128)(2,1)}, u32[]{:S(2)}) copy-start(bf16[9,144]{1,0:T(8,128)(2,1)} %param.13) | copy-start | bytes 7780
  7.2 126.8 %copy-start.6 = (bf16[1,2,64,1152]{3,2,1,0:T(8,128)(2,1)S(1)}, bf16[1,2,64,1152]{3,2,1,0:T(8,128)(2,1)}, u32[]{:S(2)}) copy-start(bf16[1,2,64,1152]{3,2,1,0:T(8,128)(2,1)} %param.8) | copy-start | bytes 884740
  7.2 137.9 %copy-start.14 = (bf16[18,216]{1,0:T(8,128)(2,1)S(1)}, bf16[18,216]{1,0:T(8,128)(2,1)}, u32[]{:S(2)}) copy-start(bf16[18,216]{1,0:T(8,128)(2,1)} %param.12) | copy-start | bytes 23332
  7.2 204.6 %all-gather.15.cloned.1.call-start = ((), (), s32[]{:S(2)}) async-start(), calls=%async_computation.6 | async-start | bytes 1492992 | tf_op jit(solution)/shard_map/all_gather | solution.py:17
  49.9 163.7 %all-gather.13.cloned.1.call-start = ((), (), s32[]{:S(2)}) async-start(), calls=%async_computation.5 | async-start | bytes 4644864 | tf_op jit(solution)/shard_map/all_gather | solution.py:17
  49.9 138.9 %copy-start.8 = (bf16[1,2,64,1152]{3,2,1,0:T(8,128)(2,1)S(1)}, bf16[1,2,64,1152]{3,2,1,0:T(8,128)(2,1)}, u32[]{:S(2)}) copy-start(bf16[1,2,64,1152]{3,2,1,0:T(8,128)(2,1)} %param.11) | copy-start | bytes 884740
  94.8 165.5 %all-gather.19.cloned.1.call-start = ((), (), s32[]{:S(2)}) async-start(), calls=%async_computation.8 | async-start | bytes 1492992 | tf_op jit(solution)/shard_map/all_gather | solution.py:17
  135.0 54.9 %all-to-all-start = ((bf16[1,2,64,1152]{3,1,0,2:T(2,128)(2,1)}), bf16[1,2,64,1152]{3,1,0,2:T(2,128)(2,1)S(1)}, u32[]{:S(2)}, u32[]{:S(2)}) async-start(bf16[1,2,64,1152]{3,1,0,2:T(2,128)(2,1)} %copy.147), calls=%async_computation | async-start | bytes 589824 | tf_op jit(solution)/shard_map/all_to_all | solution.py:84
  145.0 236.4 %all-gather.17.cloned.1.call-start = ((), (), s32[]{:S(2)}) async-start(), calls=%async_computation.7 | async-start | bytes 4644864 | tf_op jit(solution)/shard_map/all_gather | solution.py:17
  189.9 21.6 %all-to-all-start.2 = ((bf16[1,2,64,1152]{3,1,0,2:T(2,128)(2,1)}), bf16[1,2,64,1152]{3,1,0,2:T(2,128)(2,1)S(1)}, u32[]{:S(2)}, u32[]{:S(2)}) async-start(bf16[1,2,64,1152]{3,1,0,2:T(2,128)(2,1)} %copy.163), calls=%async_computation.2 | async-start | bytes 589824 | tf_op jit(solution)/shard_map/all_to_all | solution.py:98
  217.5 2.2 copy-start
  219.6 11.0 %copy-start.2 = (bf16[576,1152]{1,0:T(8,128)(2,1)S(1)}, bf16[576,1152]{1,0:T(8,128)(2,1)}, u32[]{:S(2)}) copy-start(bf16[576,1152]{1,0:T(8,128)(2,1)} %all-gather.15.cloned.1.call-done) | copy-start | bytes 3981316
  225.6 23.0 %all-to-all-start.3 = ((bf16[64,2,1152]{2,1,0:T(2,128)(2,1)}), bf16[64,2,1152]{2,1,0:T(2,128)(2,1)S(1)}, u32[]{:S(2)}, u32[]{:S(2)}) async-start(bf16[64,2,1152]{2,1,0:T(2,128)(2,1)} %reshape.534), calls=%async_computation.3 | async-start | bytes 589824 | tf_op jit(solution)/shard_map/all_to_all | solution.py:102
  239.2 21.0 %copy-start.11 = (bf16[1,2,64,1152]{3,2,1,0:T(8,128)(2,1)S(1)}, bf16[1,2,64,1152]{3,2,1,0:T(8,128)(2,1)}, u32[]{:S(2)}) copy-start(bf16[1,2,64,1152]{3,2,1,0:T(8,128)(2,1)} %param.10) | copy-start | bytes 884740
  248.6 22.1 %all-to-all-start.1 = ((bf16[64,2,1152]{2,1,0:T(2,128)(2,1)}), bf16[64,2,1152]{2,1,0:T(2,128)(2,1)S(1)}, u32[]{:S(2)}, u32[]{:S(2)}) async-start(bf16[64,2,1152]{2,1,0:T(2,128)(2,1)} %reshape.532), calls=%async_computation.1 | async-start | bytes 589824 | tf_op jit(solution)/shard_map/all_to_all | solution.py:88
  260.3 10.3 %copy-start.5 = (bf16[1,2,64,1152]{3,2,1,0:T(8,128)(2,1)}, bf16[1,2,64,1152]{3,2,1,0:T(8,128)(2,1)S(1)}, u32[]{:S(2)}) copy-start(bf16[1,2,64,1152]{3,2,1,0:T(8,128)(2,1)S(1)} %fusion.15) | copy-start | bytes 884740
  260.3 28.2 %copy-start.12 = (bf16[1,2,64,1152]{3,2,1,0:T(8,128)(2,1)S(1)}, bf16[1,2,64,1152]{3,2,1,0:T(8,128)(2,1)}, u32[]{:S(2)}) copy-start(bf16[1,2,64,1152]{3,2,1,0:T(8,128)(2,1)} %param.9) | copy-start | bytes 884740
  270.7 135.3 %all-to-all-start.4 = ((bf16[512,2,648]{2,1,0:T(2,128)(2,1)}), bf16[512,2,648]{2,1,0:T(2,128)(2,1)S(1)}, u32[]{:S(2)}, u32[]{:S(2)}) async-start(bf16[512,2,648]{2,1,0:T(2,128)(2,1)} %reshape.536), calls=%async_computation.4 | async-start | bytes 3145728 | tf_op jit(solution)/shard_map/all_to_all | solution.py:26
  288.8 98.2 %copy-start.3 = (bf16[1,2,64,1152]{3,2,1,0:T(8,128)(2,1)}, bf16[1,2,64,1152]{3,2,1,0:T(8,128)(2,1)S(1)}, u32[]{:S(2)}) copy-start(bf16[1,2,64,1152]{3,2,1,0:T(8,128)(2,1)S(1)} %get-tuple-element.14) | copy-start | bytes 884740
  388.9 1.6 copy-start.13
  396.4 8.1 %copy-start.1 = (bf16[576,1152]{1,0:T(8,128)(2,1)S(1)}, bf16[576,1152]{1,0:T(8,128)(2,1)}, u32[]{:S(2)}) copy-start(bf16[576,1152]{1,0:T(8,128)(2,1)} %all-gather.19.cloned.1.call-done) | copy-start | bytes 3981316
  397.7 6.6 %copy-start.4 = (bf16[1,2,64,1152]{3,2,1,0:T(8,128)(2,1)S(1)}, bf16[1,2,64,1152]{3,2,1,0:T(8,128)(2,1)}, u32[]{:S(2)}) copy-start(bf16[1,2,64,1152]{3,2,1,0:T(8,128)(2,1)} %copy-done.3) | copy-start | bytes 884740
  398.6 6.3 %copy-start.7 = (bf16[1,2,64,1152]{3,2,1,0:T(8,128)(2,1)S(1)}, bf16[1,2,64,1152]{3,2,1,0:T(8,128)(2,1)}, u32[]{:S(2)}) copy-start(bf16[1,2,64,1152]{3,2,1,0:T(8,128)(2,1)} %param.8) | copy-start | bytes 884740
  400.5 4.0 copy-start.10
  400.5 4.4 %copy-start.9 = (bf16[1,2,64,1152]{3,2,1,0:T(8,128)(2,1)S(1)}, bf16[1,2,64,1152]{3,2,1,0:T(8,128)(2,1)}, u32[]{:S(2)}) copy-start(bf16[1,2,64,1152]{3,2,1,0:T(8,128)(2,1)} %param.11) | copy-start | bytes 884740
Sparse Core Ops, SparseCore 0:
  50.0 45.1 all-gather.14
  97.3 101.8 all-gather.12
  201.9 44.7 all-gather.18
  248.6 132.7 all-gather.16

commit v6 on v4

--- a/solution.py
+++ b/solution.py
@@ -18,11 +18,12 @@
     return shard
 
 
-def scatter_grad(partial):
-    rows, cols = partial.shape
+def scatter_grad(mixed, cot):
     dp, seq = lax.axis_size(DP), lax.axis_size(SEQ)
-    blocks = partial.reshape(seq, rows // seq, dp, cols // dp).transpose(2, 0, 1, 3)
-    blocks = blocks.reshape(dp * seq, rows // seq, cols // dp)
+    mixed = mixed.reshape(-1, seq, mixed.shape[-1] // seq)
+    cot = cot.reshape(-1, dp, cot.shape[-1] // dp)
+    blocks = jnp.einsum("tsr,tdc->dsrc", mixed, cot, preferred_element_type=jnp.float32)
+    blocks = blocks.reshape(dp * seq, mixed.shape[-1], cot.shape[-1])
     sent = lax.all_to_all(blocks.astype(jnp.bfloat16), DP + SEQ, 0, 0, tiled=True)
     return sent.astype(jnp.float32).sum(0)
 
@@ -109,13 +110,9 @@
     second_grad = (
         grad_second.astype(jnp.float32) + back_space.reshape(y_first.shape).astype(jnp.float32)
     ).astype(jnp.bfloat16)
-    partial_grad = lax.dot_general(
-        time_mixed.reshape(-1, time_mixed.shape[3]),
-        cot_patch.reshape(-1, width),
-        (((0,), (0,)), ((), ())),
-        preferred_element_type=jnp.float32,
+    grad_share = scatter_grad(
+        time_mixed.reshape(-1, time_mixed.shape[3]), cot_patch.reshape(-1, width)
     )
-    grad_share = scatter_grad(partial_grad)
     return (first_in, second_in, first_grad, second_grad, grad_share)
 
 

time: 390 us -> 391 us (level)
    all_to_all x1, starting transfers between devices: 4.91 us -> 9.95 us  [body(): lax.all_to_all(for_sending(back_patch), SEQ, split_axis=1, concat_axis=2,...]
    all_to_all x1, starting transfers between devices: 9.59 us -> 4.62 us  [body(): lax.all_to_all(y_first, SEQ, split_axis=2, concat_axis=1, tiled=True)]
where the time goes in v6:
time: 391 us; the launch traced here: 385 us
  blocking collectives  199 us (51%)
  starting transfers between devices  56 us (14%)
  local copies, waits for them, and re-layouts  42 us (11%)
  waiting for transfers between devices  36 us (9%)
  matrix products  24.8 us (6%)
  between operations  14.9 us (4%)
  other arithmetic  12.9 us (3%)
    all_gather x16, blocking collectives, gather_weight(): shard = lax.all_gather(shard, axis, axis=dim, tiled=True)  199 us
    unnamed x57, local copies, waits for them, and re-layouts  25.7 us
    all_to_all x1, starting transfers between devices, scatter_grad(): lax.all_to_all(blocks.astype(jnp.bfloat16), DP + SEQ, 0, 0, tiled=True)  20.9 us
    all_to_all x1, waiting for transfers between devices, scatter_grad(): lax.all_to_all(blocks.astype(jnp.bfloat16), DP + SEQ, 0, 0, tiled=True)  18.6 us
    dot_general x4, matrix products, attend(): jnp.dot(normed, w_qkv, preferred_element_type=jnp.float32)  12.9 us
    all_to_all x1, starting transfers between devices, body(): lax.all_to_all(for_sending(time_out), SEQ, split_axis=1, concat_axis=2, t...  10.8 us
    all_to_all x1, waiting for transfers between devices, body(): lax.all_to_all(grad_second, SEQ, split_axis=2, concat_axis=1, tiled=True)  10.2 us
    all_to_all x1, starting transfers between devices, body(): lax.all_to_all(for_sending(back_patch), SEQ, split_axis=1, concat_axis=2,...  9.95 us
  transfers between devices with their start and end apart: 9, of which 3 were waited for; matrix products, arithmetic and copies ran while one was open for 17% of the time, Pallas kernels for 0%

profile of v6, /device:TPU:1, one launch (start us, length us, event | category | flops | bytes accessed | tf_op | source)
XLA Modules:
  0.0 385.5 jit_solution(5109790437291305257)
XLA Ops:
  7.2 8.5 %all-gather.3 = bf16[2,144,9]{1,2,0:T(8,128)(2,1)S(1)} all-gather(bf16[1,144,9]{1,2,0:T(8,128)(2,1)} %bitcast.263), channel_id=1, replica_groups=mesh['zh'=4,'core'=2,'x'=4,'zl'=2,'y'=8] {'core'}, dimensions={0}, use_global_device_ids=true | all-gather | bytes 7776 | tf_op jit(solution)/shard_map/all_gather | solution.py:17
  15.9 11.2 %all-gather.4 = bf16[4,288,9]{1,2,0:T(8,128)(2,1)S(1)} all-gather(bf16[1,288,9]{1,2,0:T(8,128)(2,1)S(1)} %reshape.521), channel_id=1, replica_groups=mesh['zh'=4,'core'=2,'x'=4,'zl'=2,'y'=8] {'zh'}, dimensions={0}, use_global_device_ids=true | all-gather | bytes 25920 | tf_op jit(solution)/shard_map/all_gather | solution.py:17
  27.1 20.5 %all-gather.5 = bf16[8,9,1152]{2,1,0:T(8,128)(2,1)S(1)} all-gather(bf16[1,9,1152]{2,1,0:T(8,128)(2,1)S(1)} %bitcast.259), channel_id=1, replica_groups=mesh['zh'=4,'core'=2,'x'=4,'zl'=2,'y'=8] {'y'}, dimensions={0}, use_global_device_ids=true | all-gather | bytes 186624 | tf_op jit(solution)/shard_map/all_gather | solution.py:17
  47.7 5.2 %all_gather.68 = bf16[144,1152]{1,0:T(8,128)(2,1)} all-gather(bf16[72,1152]{1,0:T(8,128)(2,1)S(1)} %reshape.524), channel_id=1, replica_groups=mesh['zh'=4,'core'=2,'x'=4,'zl'=2,'y'=8] {'zl'}, dimensions={0}, use_global_device_ids=true | all-gather | bytes 497664 | tf_op jit(solution)/shard_map/all_gather | solution.py:17
  52.9 11.7 %all-gather = bf16[2,216,18]{1,2,0:T(8,128)(2,1)S(1)} all-gather(bf16[1,216,18]{1,2,0:T(8,128)(2,1)} %bitcast.261), channel_id=1, replica_groups=mesh['zh'=4,'core'=2,'x'=4,'zl'=2,'y'=8] {'core'}, dimensions={0}, use_global_device_ids=true | all-gather | bytes 23328 | tf_op jit(solution)/shard_map/all_gather | solution.py:17
  64.8 11.2 %all-gather.1 = bf16[4,432,18]{1,2,0:T(8,128)(2,1)S(1)} all-gather(bf16[1,432,18]{1,2,0:T(8,128)(2,1)S(1)} %reshape.515), channel_id=1, replica_groups=mesh['zh'=4,'core'=2,'x'=4,'zl'=2,'y'=8] {'zh'}, dimensions={0}, use_global_device_ids=true | all-gather | bytes 77760 | tf_op jit(solution)/shard_map/all_gather | solution.py:17
  76.2 21.8 %all-gather.2 = bf16[8,18,1728]{2,1,0:T(8,128)(2,1)S(1)} all-gather(bf16[1,18,1728]{2,1,0:T(8,128)(2,1)S(1)} %bitcast.255), channel_id=1, replica_groups=mesh['zh'=4,'core'=2,'x'=4,'zl'=2,'y'=8] {'y'}, dimensions={0}, use_global_device_ids=true | all-gather | bytes 559872 | tf_op jit(solution)/shard_map/all_gather | solution.py:17
  98.3 8.7 %all_gather.63 = bf16[288,1728]{1,0:T(8,128)(2,1)} all-gather(bf16[144,1728]{1,0:T(8,128)(2,1)S(1)} %reshape.518), channel_id=1, replica_groups=mesh['zh'=4,'core'=2,'x'=4,'zl'=2,'y'=8] {'zl'}, dimensions={0}, use_global_device_ids=true | all-gather | bytes 1492992 | tf_op jit(solution)/shard_map/all_gather | solution.py:17
  107.1 9.7 %all-gather.9 = bf16[2,144,9]{1,2,0:T(8,128)(2,1)S(1)} all-gather(bf16[1,144,9]{1,2,0:T(8,128)(2,1)S(1)} %bitcast.264), channel_id=1, replica_groups=mesh['zh'=4,'core'=2,'x'=4,'zl'=2,'y'=8] {'core'}, dimensions={0}, use_global_device_ids=true | all-gather | bytes 7776 | tf_op jit(solution)/shard_map/all_gather | solution.py:17
  116.9 11.0 %all-gather.10 = bf16[4,288,9]{1,2,0:T(8,128)(2,1)S(1)} all-gather(bf16[1,288,9]{1,2,0:T(8,128)(2,1)S(1)} %reshape.533), channel_id=1, replica_groups=mesh['zh'=4,'core'=2,'x'=4,'zl'=2,'y'=8] {'zh'}, dimensions={0}, use_global_device_ids=true | all-gather | bytes 25920 | tf_op jit(solution)/shard_map/all_gather | solution.py:17
  128.0 21.3 %all-gather.11 = bf16[8,9,1152]{2,1,0:T(8,128)(2,1)S(1)} all-gather(bf16[1,9,1152]{2,1,0:T(8,128)(2,1)S(1)} %bitcast.260), channel_id=1, replica_groups=mesh['zh'=4,'core'=2,'x'=4,'zl'=2,'y'=8] {'y'}, dimensions={0}, use_global_device_ids=true | all-gather | bytes 186624 | tf_op jit(solution)/shard_map/all_gather | solution.py:17
  149.3 5.3 %all_gather.78 = bf16[144,1152]{1,0:T(8,128)(2,1)} all-gather(bf16[72,1152]{1,0:T(8,128)(2,1)S(1)} %reshape.536), channel_id=1, replica_groups=mesh['zh'=4,'core'=2,'x'=4,'zl'=2,'y'=8] {'zl'}, dimensions={0}, use_global_device_ids=true | all-gather | bytes 497664 | tf_op jit(solution)/shard_map/all_gather | solution.py:17
  154.6 1.0 copy.213
  155.7 9.6 %all-to-all-start.2 = ((bf16[1,2,64,1152]{3,1,0,2:T(2,128)(2,1)}), bf16[1,2,64,1152]{3,1,0,2:T(2,128)(2,1)S(1)}, u32[]{:S(2)}, u32[]{:S(2)}) async-start(bf16[1,2,64,1152]{3,1,0,2:T(2,128)(2,1)} %copy.213), calls=%async_computation.2 | async-start | bytes 589824 | tf_op jit(solution)/shard_map/all_to_all | solution.py:99
  165.3 1.0 copy.193
  166.3 10.2 %all-to-all-done.2 = bf16[1,2,64,1152]{3,1,0,2:T(2,128)(2,1)S(1)} async-done(((bf16[1,2,64,1152]{3,1,0,2:T(2,128)(2,1)}), bf16[1,2,64,1152]{3,1,0,2:T(2,128)(2,1)S(1)}, u32[]{:S(2)}, u32[]{:S(2)}) %all-to-all-start.2) | async-done | bytes 294944 | tf_op jit(solution)/shard_map/all_to_all | solution.py:99
  176.5 4.6 %all-to-all-start = ((bf16[1,2,64,1152]{3,1,0,2:T(2,128)(2,1)}), bf16[1,2,64,1152]{3,1,0,2:T(2,128)(2,1)S(1)}, u32[]{:S(2)}, u32[]{:S(2)}) async-start(bf16[1,2,64,1152]{3,1,0,2:T(2,128)(2,1)} %copy.193), calls=%async_computation | async-start | bytes 589824 | tf_op jit(solution)/shard_map/all_to_all | solution.py:85
  181.2 10.6 %all-gather.6 = bf16[2,216,18]{1,2,0:T(8,128)(2,1)S(1)} all-gather(bf16[1,216,18]{1,2,0:T(8,128)(2,1)S(1)} %bitcast.262), channel_id=1, replica_groups=mesh['zh'=4,'core'=2,'x'=4,'zl'=2,'y'=8] {'core'}, dimensions={0}, use_global_device_ids=true | all-gather | bytes 23328 | tf_op jit(solution)/shard_map/all_gather | solution.py:17
  191.9 11.7 %all-gather.7 = bf16[4,432,18]{1,2,0:T(8,128)(2,1)S(1)} all-gather(bf16[1,432,18]{1,2,0:T(8,128)(2,1)S(1)} %reshape.527), channel_id=1, replica_groups=mesh['zh'=4,'core'=2,'x'=4,'zl'=2,'y'=8] {'zh'}, dimensions={0}, use_global_device_ids=true | all-gather | bytes 77760 | tf_op jit(solution)/shard_map/all_gather | solution.py:17
  203.8 21.6 %all-gather.8 = bf16[8,18,1728]{2,1,0:T(8,128)(2,1)S(1)} all-gather(bf16[1,18,1728]{2,1,0:T(8,128)(2,1)S(1)} %bitcast.256), channel_id=1, replica_groups=mesh['zh'=4,'core'=2,'x'=4,'zl'=2,'y'=8] {'y'}, dimensions={0}, use_global_device_ids=true | all-gather | bytes 559872 | tf_op jit(solution)/shard_map/all_gather | solution.py:17
  225.7 8.9 %all_gather.73 = bf16[288,1728]{1,0:T(8,128)(2,1)} all-gather(bf16[144,1728]{1,0:T(8,128)(2,1)S(1)} %reshape.530), channel_id=1, replica_groups=mesh['zh'=4,'core'=2,'x'=4,'zl'=2,'y'=8] {'zl'}, dimensions={0}, use_global_device_ids=true | all-gather | bytes 1492992 | tf_op jit(solution)/shard_map/all_gather | solution.py:17
  237.4 1.8 convolution_convert_fusion.18
  239.2 3.8 convolution_convert_fusion.5
  245.3 1.5 multiply_reduce_fusion
  247.9 2.4 reduce.29
  251.2 9.9 %all-to-all-start.3 = ((bf16[64,2,1152]{2,1,0:T(2,128)(2,1)}), bf16[64,2,1152]{2,1,0:T(2,128)(2,1)S(1)}, u32[]{:S(2)}, u32[]{:S(2)}) async-start(bf16[64,2,1152]{2,1,0:T(2,128)(2,1)} %reshape.546), calls=%async_computation.3 | async-start | bytes 589824 | tf_op jit(solution)/shard_map/all_to_all | solution.py:103
  262.3 2.4 reduce.28
  266.4 3.5 copy.226
  269.9 9.3 %reshape.548 = bf16[512,2,648]{2,1,0:T(2,128)(2,1)} reshape(bf16[512,9,144]{2,1,0:T(8,128)(2,1)} %copy.226) | data formatting | bytes 2654208
  279.3 10.8 %all-to-all-start.1 = ((bf16[64,2,1152]{2,1,0:T(2,128)(2,1)}), bf16[64,2,1152]{2,1,0:T(2,128)(2,1)S(1)}, u32[]{:S(2)}, u32[]{:S(2)}) async-start(bf16[64,2,1152]{2,1,0:T(2,128)(2,1)} %reshape.544), calls=%async_computation.1 | async-start | bytes 589824 | tf_op jit(solution)/shard_map/all_to_all | solution.py:89
  291.1 2.0 convolution_convert_fusion.17
  293.2 1.0 reshape.498
  294.2 7.1 %all-to-all-done.1 = bf16[64,2,1152]{2,1,0:T(2,128)(2,1)S(1)} async-done(((bf16[64,2,1152]{2,1,0:T(2,128)(2,1)}), bf16[64,2,1152]{2,1,0:T(2,128)(2,1)S(1)}, u32[]{:S(2)}, u32[]{:S(2)}) %all-to-all-start.1) | async-done | bytes 294944 | tf_op jit(solution)/shard_map/all_to_all | solution.py:89
  301.3 20.9 %all-to-all-start.4 = ((bf16[512,2,648]{2,1,0:T(2,128)(2,1)}), bf16[512,2,648]{2,1,0:T(2,128)(2,1)S(1)}, u32[]{:S(2)}, u32[]{:S(2)}) async-start(bf16[512,2,648]{2,1,0:T(2,128)(2,1)} %reshape.548), calls=%async_computation.4 | async-start | bytes 3145728 | tf_op jit(solution)/shard_map/all_to_all | solution.py:27
  323.5 3.8 convolution_convert_fusion.3
  327.7 1.3 fusion.59
  329.9 1.2 copy.238
  331.0 1.4 convert_reduce_fusion.1
  333.2 1.2 fusion.6
  334.6 1.4 copy.223
  336.0 2.5 reshape.500
  338.5 1.3 fusion.5
  340.7 1.9 reshape.493
  342.7 3.8 fusion
  347.1 1.1 fusion.16
  348.2 18.6 %all-to-all-done.4 = bf16[512,2,648]{2,1,0:T(2,128)(2,1)S(1)} async-done(((bf16[512,2,648]{2,1,0:T(2,128)(2,1)}), bf16[512,2,648]{2,1,0:T(2,128)(2,1)S(1)}, u32[]{:S(2)}, u32[]{:S(2)}) %all-to-all-start.4) | async-done | bytes 1327136 | tf_op jit(solution)/shard_map/all_to_all | solution.py:27
  366.7 8.1 %reshape.549 = bf16[512,9,144]{2,1,0:T(8,128)(2,1)} reshape(bf16[512,2,648]{2,1,0:T(2,128)(2,1)S(1)} %all-to-all-done.4) | data formatting | bytes 2654208
  374.8 3.7 convert_reduce_fusion
  (125 shorter events, 17.5 us)
Async XLA Ops:
  7.2 99.9 %copy-start.15 = (bf16[9,144]{1,0:T(8,128)(2,1)S(1)}, bf16[9,144]{1,0:T(8,128)(2,1)}, u32[]{:S(2)}) copy-start(bf16[9,144]{1,0:T(8,128)(2,1)} %param.13) | copy-start | bytes 7780
  7.2 230.2 %all-gather.19.cloned.1.call-start = ((), (), s32[]{:S(2)}) async-start(), calls=%async_computation.6 | async-start | bytes 1658880 | tf_op jit(solution)/shard_map/all_gather | solution.py:17
  47.6 107.0 %copy-start.8 = (bf16[1,2,64,1152]{3,2,1,0:T(8,128)(2,1)S(1)}, bf16[1,2,64,1152]{3,2,1,0:T(8,128)(2,1)}, u32[]{:S(2)}) copy-start(bf16[1,2,64,1152]{3,2,1,0:T(8,128)(2,1)} %param.11) | copy-start | bytes 884740
  52.9 112.4 %copy-start.6 = (bf16[1,2,64,1152]{3,2,1,0:T(8,128)(2,1)S(1)}, bf16[1,2,64,1152]{3,2,1,0:T(8,128)(2,1)}, u32[]{:S(2)}) copy-start(bf16[1,2,64,1152]{3,2,1,0:T(8,128)(2,1)} %param.8) | copy-start | bytes 884740
  52.9 186.3 %all-gather.17.cloned.1.call-start = ((), (), s32[]{:S(2)}) async-start(), calls=%async_computation.5 | async-start | bytes 5160960 | tf_op jit(solution)/shard_map/all_gather | solution.py:17
  98.0 83.2 %copy-start.14 = (bf16[18,216]{1,0:T(8,128)(2,1)S(1)}, bf16[18,216]{1,0:T(8,128)(2,1)}, u32[]{:S(2)}) copy-start(bf16[18,216]{1,0:T(8,128)(2,1)} %param.12) | copy-start | bytes 23332
  107.0 184.1 %all-gather.23.cloned.1.call-start = ((), (), s32[]{:S(2)}) async-start(), calls=%async_computation.8 | async-start | bytes 1658880 | tf_op jit(solution)/shard_map/all_gather | solution.py:17
  155.7 20.9 %all-to-all-start.2 = ((bf16[1,2,64,1152]{3,1,0,2:T(2,128)(2,1)}), bf16[1,2,64,1152]{3,1,0,2:T(2,128)(2,1)S(1)}, u32[]{:S(2)}, u32[]{:S(2)}) async-start(bf16[1,2,64,1152]{3,1,0,2:T(2,128)(2,1)} %copy.213), calls=%async_computation.2 | async-start | bytes 589824 | tf_op jit(solution)/shard_map/all_to_all | solution.py:99
  176.5 59.1 %all-to-all-start = ((bf16[1,2,64,1152]{3,1,0,2:T(2,128)(2,1)}), bf16[1,2,64,1152]{3,1,0,2:T(2,128)(2,1)S(1)}, u32[]{:S(2)}, u32[]{:S(2)}) async-start(bf16[1,2,64,1152]{3,1,0,2:T(2,128)(2,1)} %copy.193), calls=%async_computation | async-start | bytes 589824 | tf_op jit(solution)/shard_map/all_to_all | solution.py:85
  181.2 142.4 %all-gather.21.cloned.1.call-start = ((), (), s32[]{:S(2)}) async-start(), calls=%async_computation.7 | async-start | bytes 5160960 | tf_op jit(solution)/shard_map/all_gather | solution.py:17
  243.1 2.2 copy-start
  245.3 16.1 %copy-start.2 = (bf16[576,1152]{1,0:T(8,128)(2,1)S(1)}, bf16[576,1152]{1,0:T(8,128)(2,1)}, u32[]{:S(2)}) copy-start(bf16[576,1152]{1,0:T(8,128)(2,1)} %all-gather.19.cloned.1.call-done) | copy-start | bytes 3981316
  251.2 28.1 %all-to-all-start.3 = ((bf16[64,2,1152]{2,1,0:T(2,128)(2,1)}), bf16[64,2,1152]{2,1,0:T(2,128)(2,1)S(1)}, u32[]{:S(2)}, u32[]{:S(2)}) async-start(bf16[64,2,1152]{2,1,0:T(2,128)(2,1)} %reshape.546), calls=%async_computation.3 | async-start | bytes 589824 | tf_op jit(solution)/shard_map/all_to_all | solution.py:103
  269.9 21.1 %copy-start.11 = (bf16[1,2,64,1152]{3,2,1,0:T(8,128)(2,1)S(1)}, bf16[1,2,64,1152]{3,2,1,0:T(8,128)(2,1)}, u32[]{:S(2)}) copy-start(bf16[1,2,64,1152]{3,2,1,0:T(8,128)(2,1)} %param.10) | copy-start | bytes 884740
  279.3 22.1 %all-to-all-start.1 = ((bf16[64,2,1152]{2,1,0:T(2,128)(2,1)}), bf16[64,2,1152]{2,1,0:T(2,128)(2,1)S(1)}, u32[]{:S(2)}, u32[]{:S(2)}) async-start(bf16[64,2,1152]{2,1,0:T(2,128)(2,1)} %reshape.544), calls=%async_computation.1 | async-start | bytes 589824 | tf_op jit(solution)/shard_map/all_to_all | solution.py:89
  291.0 10.3 %copy-start.5 = (bf16[1,2,64,1152]{3,2,1,0:T(8,128)(2,1)}, bf16[1,2,64,1152]{3,2,1,0:T(8,128)(2,1)S(1)}, u32[]{:S(2)}) copy-start(bf16[1,2,64,1152]{3,2,1,0:T(8,128)(2,1)S(1)} %fusion.15) | copy-start | bytes 884740
  291.0 32.0 %copy-start.12 = (bf16[1,2,64,1152]{3,2,1,0:T(8,128)(2,1)S(1)}, bf16[1,2,64,1152]{3,2,1,0:T(8,128)(2,1)}, u32[]{:S(2)}) copy-start(bf16[1,2,64,1152]{3,2,1,0:T(8,128)(2,1)} %param.9) | copy-start | bytes 884740
  301.3 65.4 %all-to-all-start.4 = ((bf16[512,2,648]{2,1,0:T(2,128)(2,1)}), bf16[512,2,648]{2,1,0:T(2,128)(2,1)S(1)}, u32[]{:S(2)}, u32[]{:S(2)}) async-start(bf16[512,2,648]{2,1,0:T(2,128)(2,1)} %reshape.548), calls=%async_computation.4 | async-start | bytes 3145728 | tf_op jit(solution)/shard_map/all_to_all | solution.py:27
  323.3 5.8 %copy-start.3 = (bf16[1,2,64,1152]{3,2,1,0:T(8,128)(2,1)}, bf16[1,2,64,1152]{3,2,1,0:T(8,128)(2,1)S(1)}, u32[]{:S(2)}) copy-start(bf16[1,2,64,1152]{3,2,1,0:T(8,128)(2,1)S(1)} %get-tuple-element.14) | copy-start | bytes 884740
  331.0 1.6 copy-start.13
  338.5 8.1 %copy-start.1 = (bf16[576,1152]{1,0:T(8,128)(2,1)S(1)}, bf16[576,1152]{1,0:T(8,128)(2,1)}, u32[]{:S(2)}) copy-start(bf16[576,1152]{1,0:T(8,128)(2,1)} %all-gather.23.cloned.1.call-done) | copy-start | bytes 3981316
  339.8 6.6 %copy-start.4 = (bf16[1,2,64,1152]{3,2,1,0:T(8,128)(2,1)S(1)}, bf16[1,2,64,1152]{3,2,1,0:T(8,128)(2,1)}, u32[]{:S(2)}) copy-start(bf16[1,2,64,1152]{3,2,1,0:T(8,128)(2,1)} %copy-done.3) | copy-start | bytes 884740
  340.7 6.3 %copy-start.7 = (bf16[1,2,64,1152]{3,2,1,0:T(8,128)(2,1)S(1)}, bf16[1,2,64,1152]{3,2,1,0:T(8,128)(2,1)}, u32[]{:S(2)}) copy-start(bf16[1,2,64,1152]{3,2,1,0:T(8,128)(2,1)} %param.8) | copy-start | bytes 884740
  342.6 4.0 %copy-start.10 = (bf16[128,576]{1,0:T(8,128)(2,1)S(1)}, bf16[128,576]{1,0:T(8,128)(2,1)}, u32[]{:S(2)}) copy-start(bf16[128,576]{1,0:T(8,128)(2,1)} %reshape.493) | copy-start | bytes 442372
  342.7 4.4 %copy-start.9 = (bf16[1,2,64,1152]{3,2,1,0:T(8,128)(2,1)S(1)}, bf16[1,2,64,1152]{3,2,1,0:T(8,128)(2,1)}, u32[]{:S(2)}) copy-start(bf16[1,2,64,1152]{3,2,1,0:T(8,128)(2,1)} %param.11) | copy-start | bytes 884740
Sparse Core Ops, SparseCore 0:
  53.0 36.2 all-gather.18
  107.1 58.1 all-gather.16
  167.4 33.0 all-gather.22
  234.7 63.2 all-gather.20
